TPU v7x, 32 devices: a whole 2x2x4 slice. The times are simulated.
32 devices in a mesh: groups: 2 (over x), row: 8 (over z, y), col: 2 (over core).
Axes of the slice: x: 2, y: 2, z: 4, core: 2. Of those that a mesh axis runs over, the one named last changes fastest.
Arguments:
- sky_map: bfloat16 [512, 1024, 128], P(('groups', 'row'), 'col'), parts along dimension 0, may hold values from -6 to 6
- expand_weight: bfloat16 [128, 256], replicated, may hold values from -0.5 to 0.5
- expand_bias: float32 [256], replicated, may hold values from -3 to 3
- depth_weight: float32 [3, 3, 256], replicated, may hold values from -2 to 2
- depth_bias: float32 [256], replicated, may hold values from -3 to 3
- project_weight: bfloat16 [256, 128], replicated, may hold values from -0.375 to 0.375
- project_bias: float32 [128], replicated, may hold values from -3 to 3
- norm_gain: float32 [128], replicated, may hold values from 0.1 to 1.9
- norm_bias: float32 [128], replicated, may hold values from -3 to 3
- mixing_weight: bfloat16 [128, 384], replicated
- position_bias: float32 [4, 225], replicated, may hold values from -4 to 4
- output_weight: bfloat16 [128, 128], replicated, may hold values from -0.5 to 0.5
Outputs:
- block_out: bfloat16 [512, 1024, 128], P(('groups', 'row'), 'col'), parts along dimension 0
There are 2 independent parts, one for each index of `groups`. A program takes and returns all parts, laid end to end along the dimension named above; an argument that names none is the same for every part. Nothing has to cross between parts.
All inputs are finite; a program needn't handle non-finite values.
Results may differ from a plain program's by a relative error of at most 0.023.
Values may be sent and summed in bfloat16 or wider, within the bound.
No kernel may reach another device: no remote copies, remote signals or barrier semaphores. Data moves between devices by JAX's collectives and lax.ppermute only.
A program may use at most 128 MiB of HBM per device.

v0:
```python
import jax
import jax.numpy as jnp
from jax import lax
from jax.sharding import PartitionSpec as P
from jax.experimental import pallas as pl

HEADS = 4
G = 8


def with_halo(array, sides, width):
    for axis, dim in sides:
        size, length = (lax.axis_size(axis), array.shape[dim])
        up = [(i, (i + 1) % size) for i in range(size - 1)]
        down = [(j, i) for i, j in up]
        last = lax.slice_in_dim(array, length - width, length, axis=dim)
        initial = lax.slice_in_dim(array, 0, width, axis=dim)
        before = lax.ppermute(last, axis, up)
        after = lax.ppermute(initial, axis, down)
        array = jnp.concatenate([before, array, after], axis=dim)
    return array


def gelu_tanh(values):
    return jax.nn.gelu(values, approximate=True)


def expand_layer(features, expand_weight, expand_bias):
    return gelu_tanh(
        jnp.dot(features, expand_weight, preferred_element_type=jnp.float32) + expand_bias
    ).astype(jnp.bfloat16)


def depthwise(padded, depth_weight, depth_bias, row_count, col_count):
    accumulated = jnp.zeros((row_count, col_count, padded.shape[2]), jnp.float32) + depth_bias
    for row_shift in range(3):
        for col_shift in range(3):
            accumulated = (
                accumulated
                + padded[row_shift : row_shift + row_count, col_shift : col_shift + col_count]
                * depth_weight[row_shift, col_shift]
            )
    return gelu_tanh(accumulated).astype(jnp.bfloat16)


def layer_norm(features, norm_gain, norm_bias):
    values = features.astype(jnp.float32)
    mean_value = jnp.mean(values, axis=-1, keepdims=True)
    variance = jnp.mean((values - mean_value) ** 2, axis=-1, keepdims=True)
    return ((values - mean_value) * lax.rsqrt(variance + 1e-05) * norm_gain + norm_bias).astype(
        jnp.bfloat16
    )


def grid_bias(position_bias, grid_side):
    position = jnp.arange(grid_side * grid_side, dtype=jnp.int32)
    row_of = position // grid_side
    col_of = position % grid_side
    offset_index = (row_of[:, None] - row_of[None, :] + grid_side - 1) * (2 * grid_side - 1) + (
        col_of[:, None] - col_of[None, :] + grid_side - 1
    )
    return jnp.take(position_bias, offset_index, axis=1)


def attend(projected, table, head_count):
    group_count, tokens, triple = projected.shape
    channels = triple // 3
    head_size = channels // head_count
    split_parts = projected.reshape(group_count, tokens, 3, head_count, head_size)
    query_part = split_parts[:, :, 0]
    key_part = split_parts[:, :, 1]
    value_part = split_parts[:, :, 2]
    scores = (
        jnp.einsum("nqhd,nkhd->nhqk", query_part, key_part, preferred_element_type=jnp.float32)
        * head_size ** (-0.5)
        + table[None]
    )
    probs = jax.nn.softmax(scores, axis=-1).astype(jnp.bfloat16)
    attended = jnp.einsum("nhqk,nkhd->nqhd", probs, value_part, preferred_element_type=jnp.float32)
    return attended.astype(jnp.bfloat16).reshape(group_count, tokens, channels)


def attention_kernel(x_ref, w_ref, bias_ref, o_ref):
    block, tokens, channels = x_ref.shape
    head_size = channels // HEADS
    x = x_ref[...].reshape(block * tokens, channels)
    qkv = jnp.dot(x, w_ref[...], preferred_element_type=jnp.float32).astype(jnp.bfloat16)
    query = qkv[:, :channels]
    key = qkv[:, channels : 2 * channels].reshape(block, tokens, channels)
    value = qkv[:, 2 * channels :]
    head_of = lax.broadcasted_iota(jnp.int32, (1, channels), 1) // head_size
    out = jnp.zeros((block, tokens, channels), jnp.float32)
    for head in range(HEADS):
        mask = head_of == head
        masked_query = jnp.where(mask, query, jnp.zeros_like(query)).reshape(block, tokens, channels)
        scores = (
            jnp.einsum("gtd,gud->gtu", masked_query, key, preferred_element_type=jnp.float32)
            * head_size ** (-0.5)
            + bias_ref[head][None]
        )
        shifted = jnp.exp(scores - jnp.max(scores, axis=-1, keepdims=True))
        probs = (shifted / jnp.sum(shifted, axis=-1, keepdims=True)).astype(jnp.bfloat16)
        masked_value = jnp.where(mask, value, jnp.zeros_like(value)).reshape(block, tokens, channels)
        part = jnp.einsum("gtu,gud->gtd", probs, masked_value, preferred_element_type=jnp.float32)
        out = jnp.where(mask.reshape(1, 1, channels), part, out)
    o_ref[...] = out.astype(o_ref.dtype)


def grid_attention(grouped, mixing_weight, table):
    count, tokens, channels = grouped.shape
    block = next(b for b in (32, 16, 8, 4, 2, 1) if count % b == 0)
    return pl.pallas_call(
        attention_kernel,
        grid=(count // block,),
        in_specs=[
            pl.BlockSpec((block, tokens, channels), lambda i: (i, 0, 0)),
            pl.BlockSpec(mixing_weight.shape, lambda i: (0, 0)),
            pl.BlockSpec(table.shape, lambda i: (0, 0, 0)),
        ],
        out_specs=pl.BlockSpec((block, tokens, channels), lambda i: (i, 0, 0)),
        out_shape=jax.ShapeDtypeStruct((count, tokens, channels), jnp.bfloat16),
    )(grouped, mixing_weight, table)


def pieces_of(normed, row_size, col_size, pp, span, col_count, channels):
    across = G // col_size
    inner_cols = col_count // across // col_size
    return (
        normed.reshape(row_size, pp, across, col_size, inner_cols, channels)
        .transpose(0, 3, 1, 2, 4, 5)
        .reshape(row_size * col_size, pp, across, inner_cols, channels)
    )


def expanded_window(expanded, edges, first, span):
    top, bottom, left, right = edges
    rows = jnp.concatenate([top, expanded, bottom], axis=0)[first : first + span + 2]
    return jnp.concatenate(
        [left[first : first + span + 2], rows, right[first : first + span + 2]], axis=1
    )


def expanded_edges(sky_map, expand_weight, expand_bias):
    row_size, col_size = lax.axis_size("row"), lax.axis_size("col")
    row_at, col_at = lax.axis_index("row"), lax.axis_index("col")
    row_count = sky_map.shape[0]
    up = [(i, i + 1) for i in range(row_size - 1)]
    top = lax.ppermute(sky_map[row_count - 1], "row", up)[None]
    bottom = lax.ppermute(sky_map[0], "row", [(j, i) for i, j in up])[None]
    last_col = jnp.concatenate([top[:, -1], sky_map[:, -1], bottom[:, -1]], axis=0)
    first_col = jnp.concatenate([top[:, 0], sky_map[:, 0], bottom[:, 0]], axis=0)
    right_of = [(i, i + 1) for i in range(col_size - 1)]
    left = lax.ppermute(last_col, "col", right_of)[:, None]
    right = lax.ppermute(first_col, "col", [(j, i) for i, j in right_of])[:, None]
    row_ok = jnp.concatenate(
        [
            jnp.full((1,), row_at > 0),
            jnp.full((row_count,), True),
            jnp.full((1,), row_at < row_size - 1),
        ]
    )[:, None, None]

    def grown(cells, valid):
        return jnp.where(valid, expand_layer(cells, expand_weight, expand_bias), jnp.zeros((), jnp.bfloat16))

    return (
        grown(top, row_at > 0),
        grown(bottom, row_at < row_size - 1),
        grown(left, row_ok & (col_at > 0)),
        grown(right, row_ok & (col_at < col_size - 1)),
    )


def body(
    sky_map,
    expand_weight,
    expand_bias,
    depth_weight,
    depth_bias,
    project_weight,
    project_bias,
    norm_gain,
    norm_bias,
    mixing_weight,
    position_bias,
    output_weight,
):
    row_count, col_count, channels = sky_map.shape
    row_size = lax.axis_size("row")
    expanded = expand_layer(sky_map, expand_weight, expand_bias)
    edges = expanded_edges(sky_map, expand_weight, expand_bias)
    across = G // lax.axis_size("col")
    stride = col_count // across
    table = grid_bias(position_bias, G)
    pieces = 2 if row_count % (2 * row_size) == 0 and (row_count // 2) % G == 0 else 1
    span = row_count // pieces
    col_size = lax.axis_size("col")
    sub = row_size // G
    pp = span // row_size
    inner_cols = stride // col_size
    source = expanded
    outs = []
    for piece in range(pieces):
        first = piece * span
        window = expanded_window(source, edges, first, span)
        hidden = depthwise(window, depth_weight, depth_bias, span, col_count)
        after_conv = (
            sky_map[first : first + span].astype(jnp.float32)
            + jnp.dot(hidden, project_weight, preferred_element_type=jnp.float32)
            + project_bias
        ).astype(jnp.bfloat16)
        normed = layer_norm(after_conv, norm_gain, norm_bias)
        pair = pieces_of(normed, row_size, col_size, pp, span, col_count, channels)
        if piece + 1 < pieces:
            pair, source = lax.optimization_barrier((pair, expanded))
        moved = lax.all_to_all(pair, ("row", "col"), 0, 0, tiled=True)
        grouped = (
            moved.reshape(G, sub, col_size, pp, across, inner_cols, channels)
            .transpose(1, 3, 5, 0, 2, 4, 6)
            .reshape(sub * pp * inner_cols, G * G, channels)
        )
        heads_out = grid_attention(grouped, mixing_weight, table)
        returned = (
            heads_out.reshape(sub, pp, inner_cols, G, col_size, across, channels)
            .transpose(3, 0, 4, 1, 5, 2, 6)
            .reshape(row_size * col_size, pp, across, inner_cols, channels)
        )
        returned = lax.all_to_all(returned, ("row", "col"), 0, 0, tiled=True)
        returned = (
            returned.reshape(row_size, col_size, pp, across, inner_cols, channels)
            .transpose(0, 2, 3, 1, 4, 5)
            .reshape(span, col_count, channels)
        )
        outs.append(
            (
                after_conv.astype(jnp.float32)
                + jnp.dot(returned, output_weight, preferred_element_type=jnp.float32)
            ).astype(jnp.bfloat16)
        )
    return jnp.concatenate(outs, axis=0)


def solution(mesh):
    placed = (
        P(("groups", "row"), "col", None),
        P(),
        P(),
        P(),
        P(),
        P(),
        P(),
        P(),
        P(),
        P(),
        P(),
        P(),
    )
    return jax.shard_map(
        body,
        mesh=mesh,
        in_specs=placed,
        out_specs=P(("groups", "row"), "col", None),
        check_vma=False,
    )
```

profile of v0, /device:TPU:13, one launch (start us, length us, event | category | flops | bytes accessed | tf_op | source)
XLA Modules:
  0.0 275.6 jit_solution(15175814930305194776)
XLA Ops:
  1.0 2.1 collective-permute-start.1
  3.2 4.0 %collective-permute-start = (bf16[512,128]{1,0:T(8,128)(2,1)S(1)}, bf16[512,128]{1,0:T(8,128)(2,1)S(1)}, u32[]{:S(2)}, u32[]{:S(2)}) collective-permute-start(bf16[512,128]{1,0:T(8,128)(2,1)S(1)} %get-tuple-element.12), channel_id=1, source_target_pairs={{0,2},{2,4},{4,6},{6,8},{8,10},{10,12},{12,14},{1,3},{3,5},{5,7},{... | collective-permute-start | bytes 393224 | tf_op jit(solution)/shard_map/ppermute | solution.py:148
  8.2 10.7 %fusion.7 = bf16[32,512,256]{2,1,0:T(8,128)(2,1)} fusion(bf16[32,512,128]{2,1,0:T(8,128)(2,1)} %param.12, f32[256]{0:T(256)} %param.14, bf16[128,256]{1,0:T(8,128)(2,1)S(1)} %copy-done), kind=kOutput, calls=%fused_computation.9 | convolution fusion | flops 1115684864 | bytes 12649472 | tf_op jit(solution)/shard_map/dot_general | solution.py:30
  19.0 3.1 %collective-permute-start.3 = (bf16[34,128]{1,0:T(8,128)(2,1)S(1)}, bf16[34,128]{1,0:T(8,128)(2,1)S(1)}, u32[]{:S(2)}, u32[]{:S(2)}) collective-permute-start(bf16[34,128]{1,0:T(8,128)(2,1)S(1)} %pad_maximum_fusion.8), channel_id=1, source_target_pairs={{1,0},{3,2},{5,4},{7,6},{9,8},{11,10},{13,12},{15,14},{17,16},{19,... | collective-permute-start | bytes 26120 | tf_op jit(solution)/shard_map/ppermute | solution.py:154
  24.2 3.1 %fusion.29 = bf16[18,512,256]{2,1,0:T(8,128)(2,1)S(1)} fusion(bf16[1,512,256]{2,1,0:T(8,128)(2,1)S(1)} %fusion.65, bf16[32,512,256]{2,1,0:T(8,128)(2,1)} %fusion.7), kind=kLoop, calls=%fused_computation.51 | loop fusion | flops 2359296 | bytes 13369344 | tf_op jit(solution)/shard_map/concatenate | solution.py:137
  28.4 23.1 %convert_reduce_fusion.1 = (f32[16,512]{1,0:T(8,128)S(1)}, bf16[16,512,128]{2,1,0:T(8,128)(2,1)S(1)}) fusion(f32[128]{0:T(128)S(1)} %copy-done.14, bf16[256,128]{1,0:T(8,128)(2,1)S(1)} %copy-done.11, bf16[18,512,256]{2,1,0:T(8,128)(2,1)S(1)} %fusion.29, bf16[18,1,256]{2,1,0:T(2,128)(2,1)S(1)} %copy.22, bf16[18,1,256]{2,1,0:T(2,128)(2,1)S(1)} %copy.20, ...), kind=kOutput, calls=%fused_computation.45 | convolution fusion | flops 662691840 | bytes 26098176 | tf_op jit(solution)/shard_map/dot_general | solution.py:209
  51.6 2.4 fusion.42
  54.0 2.5 fusion.45
  58.0 5.3 %all-to-all-start = ((bf16[16,2,4,64,128]{4,3,2,1,0:T(8,128)(2,1)}), bf16[16,2,4,64,128]{4,3,2,1,0:T(8,128)(2,1)}, u32[]{:S(2)}, u32[]{:S(2)}) async-start(bf16[16,2,4,64,128]{4,3,2,1,0:T(8,128)(2,1)} %bitcast.115), calls=%async_computation | async-start | bytes 4194304 | tf_op jit(solution)/shard_map/all_to_all | solution.py:216
  63.4 2.7 fusion.28
  66.9 24.7 %convert_reduce_fusion = (f32[16,512]{1,0:T(8,128)S(1)}, bf16[16,512,128]{2,1,0:T(8,128)(2,1)S(1)}) fusion(f32[128]{0:T(128)S(1)} %copy-done.14, bf16[256,128]{1,0:T(8,128)(2,1)S(1)} %copy-done.11, bf16[18,512,256]{2,1,0:T(8,128)(2,1)S(1)} %fusion.28, bf16[18,1,256]{2,1,0:T(2,128)(2,1)S(1)} %copy.30, bf16[18,1,256]{2,1,0:T(2,128)(2,1)S(1)} %copy.29, ...), kind=kOutput, calls=%fused_computation.42 | convolution fusion | flops 662691840 | bytes 26079744 | tf_op jit(solution)/shard_map/dot_general | solution.py:209
  91.7 2.4 fusion.38
  94.1 2.5 fusion.41
  98.1 12.8 %all-to-all-done = bf16[16,2,4,64,128]{4,3,2,1,0:T(8,128)(2,1)} async-done(((bf16[16,2,4,64,128]{4,3,2,1,0:T(8,128)(2,1)}), bf16[16,2,4,64,128]{4,3,2,1,0:T(8,128)(2,1)}, u32[]{:S(2)}, u32[]{:S(2)}) %all-to-all-start) | async-done | bytes 2097184 | tf_op jit(solution)/shard_map/all_to_all | solution.py:216
  110.9 4.9 %all-to-all-start.2 = ((bf16[16,2,4,64,128]{4,3,2,1,0:T(8,128)(2,1)}), bf16[16,2,4,64,128]{4,3,2,1,0:T(8,128)(2,1)}, u32[]{:S(2)}, u32[]{:S(2)}) async-start(bf16[16,2,4,64,128]{4,3,2,1,0:T(8,128)(2,1)} %bitcast.114), calls=%async_computation.2 | async-start | bytes 4194304 | tf_op jit(solution)/shard_map/all_to_all | solution.py:216
  116.1 14.2 %gather_fusion = f32[4096,4]{1,0:T(8,128)} fusion(f32[4,225]{0,1:T(8,128)S(1)} %copy.25, s32[4096]{0:T(1024)S(1)} %broadcast_clamp_fusion), kind=kCustom, calls=%fused_computation | custom fusion | bytes 147456 | tf_op jit(solution)/shard_map/jit(_take)/gather | solution.py:62
  130.3 2.3 copy.35
  133.4 4.6 %copy.24 = bf16[8,1,2,2,4,64,128]{6,4,2,0,5,3,1:T(4,128)(2,1)} copy(bf16[8,1,2,2,4,64,128]{6,5,4,3,2,0,1:T(8,128)(2,1)} %bitcast.29) | data formatting | bytes 4194304 | tf_op jit(solution)/shard_map/reshape | solution.py:218
  138.0 16.0 %shard_map.118 = bf16[128,64,128]{2,1,0:T(8,128)(2,1)} custom-call(bf16[128,64,128]{2,1,0:T(8,128)(2,1)} %bitcast.120, bf16[128,384]{1,0:T(8,128)(2,1)} %w_ref.3, f32[4,64,64]{2,1,0:T(8,128)} %select_bitcast_fusion.bias_ref), custom_call_target="tpu_custom_call" | custom-call | tf_op jit(solution)/shard_map/pallas_call | solution.py:112
  154.0 5.4 %copy.27 = bf16[8,1,2,2,4,64,128]{6,5,4,3,2,0,1:T(8,128)(2,1)} copy(bf16[8,1,2,2,4,64,128]{6,4,2,0,5,3,1:T(4,128)(2,1)} %bitcast.121) | data formatting | bytes 4194304 | tf_op jit(solution)/shard_map/transpose | solution.py:225
  159.4 3.9 %all-to-all-done.2 = bf16[16,2,4,64,128]{4,3,2,1,0:T(8,128)(2,1)} async-done(((bf16[16,2,4,64,128]{4,3,2,1,0:T(8,128)(2,1)}), bf16[16,2,4,64,128]{4,3,2,1,0:T(8,128)(2,1)}, u32[]{:S(2)}, u32[]{:S(2)}) %all-to-all-start.2) | async-done | bytes 2097184 | tf_op jit(solution)/shard_map/all_to_all | solution.py:216
  163.3 4.9 %all-to-all-start.1 = ((bf16[16,2,4,64,128]{4,3,2,1,0:T(8,128)(2,1)}), bf16[16,2,4,64,128]{4,3,2,1,0:T(8,128)(2,1)}, u32[]{:S(2)}, u32[]{:S(2)}) async-start(bf16[16,2,4,64,128]{4,3,2,1,0:T(8,128)(2,1)} %bitcast.116), calls=%async_computation.1 | async-start | bytes 4194304 | tf_op jit(solution)/shard_map/all_to_all | solution.py:228
  168.3 4.6 %copy.32 = bf16[8,1,2,2,4,64,128]{6,4,2,0,5,3,1:T(4,128)(2,1)} copy(bf16[8,1,2,2,4,64,128]{6,5,4,3,2,0,1:T(8,128)(2,1)} %bitcast.47) | data formatting | bytes 4194304 | tf_op jit(solution)/shard_map/reshape | solution.py:218
  172.9 16.0 %shard_map.119 = bf16[128,64,128]{2,1,0:T(8,128)(2,1)} custom-call(bf16[128,64,128]{2,1,0:T(8,128)(2,1)} %bitcast.118, bf16[128,384]{1,0:T(8,128)(2,1)} %w_ref.3, f32[4,64,64]{2,1,0:T(8,128)} %select_bitcast_fusion.bias_ref), custom_call_target="tpu_custom_call" | custom-call | tf_op jit(solution)/shard_map/pallas_call | solution.py:112
  188.8 5.4 %copy.33 = bf16[8,1,2,2,4,64,128]{6,5,4,3,2,0,1:T(8,128)(2,1)} copy(bf16[8,1,2,2,4,64,128]{6,4,2,0,5,3,1:T(4,128)(2,1)} %bitcast.119) | data formatting | bytes 4194304 | tf_op jit(solution)/shard_map/transpose | solution.py:225
  194.2 21.6 %all-to-all-done.1 = bf16[16,2,4,64,128]{4,3,2,1,0:T(8,128)(2,1)} async-done(((bf16[16,2,4,64,128]{4,3,2,1,0:T(8,128)(2,1)}), bf16[16,2,4,64,128]{4,3,2,1,0:T(8,128)(2,1)}, u32[]{:S(2)}, u32[]{:S(2)}) %all-to-all-start.1) | async-done | bytes 2097184 | tf_op jit(solution)/shard_map/all_to_all | solution.py:228
  215.8 4.9 %all-to-all-start.3 = ((bf16[16,2,4,64,128]{4,3,2,1,0:T(8,128)(2,1)}), bf16[16,2,4,64,128]{4,3,2,1,0:T(8,128)(2,1)}, u32[]{:S(2)}, u32[]{:S(2)}) async-start(bf16[16,2,4,64,128]{4,3,2,1,0:T(8,128)(2,1)} %bitcast.117), calls=%async_computation.3 | async-start | bytes 4194304 | tf_op jit(solution)/shard_map/all_to_all | solution.py:228
  220.7 3.2 %copy.28 = bf16[8,2,4,2,64,128]{5,4,3,2,1,0:T(8,128)(2,1)} copy(bf16[8,2,4,2,64,128]{5,4,2,1,3,0:T(8,128)(2,1)} %bitcast.38) | data formatting | bytes 4194304 | tf_op jit(solution)/shard_map/transpose | solution.py:231
  223.9 44.3 %all-to-all-done.3 = bf16[16,2,4,64,128]{4,3,2,1,0:T(8,128)(2,1)} async-done(((bf16[16,2,4,64,128]{4,3,2,1,0:T(8,128)(2,1)}), bf16[16,2,4,64,128]{4,3,2,1,0:T(8,128)(2,1)}, u32[]{:S(2)}, u32[]{:S(2)}) %all-to-all-start.3) | async-done | bytes 2097184 | tf_op jit(solution)/shard_map/all_to_all | solution.py:228
  268.2 1.9 copy.34
  270.1 2.3 fusion.46
  273.2 2.4 pad_maximum_fusion.6
  (75 shorter events, 10.7 us)
Async XLA Ops:
  0.0 8.1 %copy-start = (bf16[128,256]{1,0:T(8,128)(2,1)S(1)}, bf16[128,256]{1,0:T(8,128)(2,1)}, u32[]{:S(2)}) copy-start(bf16[128,256]{1,0:T(8,128)(2,1)} %param.13) | copy-start | bytes 196612
  1.0 17.9 %collective-permute-start.1 = (bf16[512,128]{1,0:T(8,128)(2,1)S(1)}, bf16[512,128]{1,0:T(8,128)(2,1)S(1)}, u32[]{:S(2)}, u32[]{:S(2)}) collective-permute-start(bf16[512,128]{1,0:T(8,128)(2,1)S(1)} %get-tuple-element.11), channel_id=1, source_target_pairs={{2,0},{4,2},{6,4},{8,6},{10,8},{12,10},{14,12},{3,1},{5,3},{7,5},{... | collective-permute-start | bytes 393224 | tf_op jit(solution)/shard_map/ppermute | solution.py:149
  3.2 15.8 %collective-permute-start = (bf16[512,128]{1,0:T(8,128)(2,1)S(1)}, bf16[512,128]{1,0:T(8,128)(2,1)S(1)}, u32[]{:S(2)}, u32[]{:S(2)}) collective-permute-start(bf16[512,128]{1,0:T(8,128)(2,1)S(1)} %get-tuple-element.12), channel_id=1, source_target_pairs={{0,2},{2,4},{4,6},{6,8},{8,10},{10,12},{12,14},{1,3},{3,5},{5,7},{... | collective-permute-start | bytes 393224 | tf_op jit(solution)/shard_map/ppermute | solution.py:148
  8.1 10.7 %copy-start.7 = (f32[3,3,256]{2,1,0:T(4,128)S(1)}, f32[3,3,256]{2,1,0:T(4,128)}, u32[]{:S(2)}) copy-start(f32[3,3,256]{2,1,0:T(4,128)} %param.15) | copy-start | bytes 27652
  8.2 15.6 %copy-start.12 = (f32[256]{0:T(256)S(1)}, f32[256]{0:T(256)}, u32[]{:S(2)}) copy-start(f32[256]{0:T(256)} %param.14) | copy-start | bytes 3076
  19.0 8.6 %collective-permute-start.3 = (bf16[34,128]{1,0:T(8,128)(2,1)S(1)}, bf16[34,128]{1,0:T(8,128)(2,1)S(1)}, u32[]{:S(2)}, u32[]{:S(2)}) collective-permute-start(bf16[34,128]{1,0:T(8,128)(2,1)S(1)} %pad_maximum_fusion.8), channel_id=1, source_target_pairs={{1,0},{3,2},{5,4},{7,6},{9,8},{11,10},{13,12},{15,14},{17,16},{19,... | collective-permute-start | bytes 26120 | tf_op jit(solution)/shard_map/ppermute | solution.py:154
  22.2 5.9 %slice-start = ((s8[8388608]{0:T(1024)(128)(4,1)}), s8[4194304]{0:T(1024)(128)(4,1)S(1)}, s32[]{:S(2)}) async-start(s8[8388608]{0:T(1024)(128)(4,1)} %bitcast.108), calls=%async_computation.4 | async-start | bytes 8388608
  22.2 5.9 %copy-start.5 = (bf16[32,512,128]{2,1,0:T(8,128)(2,1)S(1)}, bf16[32,512,128]{2,1,0:T(8,128)(2,1)}, u32[]{:S(2)}) copy-start(bf16[32,512,128]{2,1,0:T(8,128)(2,1)} %param.12) | copy-start | bytes 12582916
  22.2 5.9 %copy-start.11 = (bf16[256,128]{1,0:T(8,128)(2,1)S(1)}, bf16[256,128]{1,0:T(8,128)(2,1)}, u32[]{:S(2)}) copy-start(bf16[256,128]{1,0:T(8,128)(2,1)} %param.17) | copy-start | bytes 196612
  22.2 5.9 %copy-start.13 = (f32[256]{0:T(256)S(1)}, f32[256]{0:T(256)}, u32[]{:S(2)}) copy-start(f32[256]{0:T(256)} %param.16) | copy-start | bytes 3076
  22.2 5.9 %copy-start.14 = (f32[128]{0:T(128)S(1)}, f32[128]{0:T(128)}, u32[]{:S(2)}) copy-start(f32[128]{0:T(128)} %param.18) | copy-start | bytes 1540
  22.2 5.6 %collective-permute-start.2 = (bf16[34,128]{1,0:T(8,128)(2,1)S(1)}, bf16[34,128]{1,0:T(8,128)(2,1)S(1)}, u32[]{:S(2)}, u32[]{:S(2)}) collective-permute-start(bf16[34,128]{1,0:T(8,128)(2,1)S(1)} %pad_maximum_fusion.7), channel_id=1, source_target_pairs={{0,1},{2,3},{4,5},{6,7},{8,9},{10,11},{12,13},{14,15},{16,17},{18,... | collective-permute-start | bytes 26120 | tf_op jit(solution)/shard_map/ppermute | solution.py:153
  24.2 4.3 %slice-start.1 = ((s8[8388608]{0:T(1024)(128)(4,1)}), s8[4194304]{0:T(1024)(128)(4,1)S(1)}, s32[]{:S(2)}) async-start(s8[8388608]{0:T(1024)(128)(4,1)} %bitcast.108), calls=%async_computation.5 | async-start | bytes 8388608
  28.4 25.5 %copy-start.9 = (f32[128]{0:T(128)S(1)}, f32[128]{0:T(128)}, u32[]{:S(2)}) copy-start(f32[128]{0:T(128)} %param.20) | copy-start | bytes 1540
  28.4 25.6 %copy-start.10 = (f32[128]{0:T(128)S(1)}, f32[128]{0:T(128)}, u32[]{:S(2)}) copy-start(f32[128]{0:T(128)} %param.19) | copy-start | bytes 1540
  58.0 52.9 %all-to-all-start = ((bf16[16,2,4,64,128]{4,3,2,1,0:T(8,128)(2,1)}), bf16[16,2,4,64,128]{4,3,2,1,0:T(8,128)(2,1)}, u32[]{:S(2)}, u32[]{:S(2)}) async-start(bf16[16,2,4,64,128]{4,3,2,1,0:T(8,128)(2,1)} %bitcast.115), calls=%async_computation | async-start | bytes 4194304 | tf_op jit(solution)/shard_map/all_to_all | solution.py:216
  63.4 3.5 %copy-start.6 = (bf16[32,512,128]{2,1,0:T(8,128)(2,1)S(1)}, bf16[32,512,128]{2,1,0:T(8,128)(2,1)}, u32[]{:S(2)}) copy-start(bf16[32,512,128]{2,1,0:T(8,128)(2,1)} %param.12) | copy-start | bytes 12582916
  91.6 2.5 copy-start.2
  91.7 24.3 %copy-start.8 = (f32[4,225]{1,0:T(4,128)S(1)}, f32[4,225]{1,0:T(4,128)}, u32[]{:S(2)}) copy-start(f32[4,225]{1,0:T(4,128)} %param.22) | copy-start | bytes 10804
  110.9 52.4 %all-to-all-start.2 = ((bf16[16,2,4,64,128]{4,3,2,1,0:T(8,128)(2,1)}), bf16[16,2,4,64,128]{4,3,2,1,0:T(8,128)(2,1)}, u32[]{:S(2)}, u32[]{:S(2)}) async-start(bf16[16,2,4,64,128]{4,3,2,1,0:T(8,128)(2,1)} %bitcast.114), calls=%async_computation.2 | async-start | bytes 4194304 | tf_op jit(solution)/shard_map/all_to_all | solution.py:216
  163.3 52.4 %all-to-all-start.1 = ((bf16[16,2,4,64,128]{4,3,2,1,0:T(8,128)(2,1)}), bf16[16,2,4,64,128]{4,3,2,1,0:T(8,128)(2,1)}, u32[]{:S(2)}, u32[]{:S(2)}) async-start(bf16[16,2,4,64,128]{4,3,2,1,0:T(8,128)(2,1)} %bitcast.116), calls=%async_computation.1 | async-start | bytes 4194304 | tf_op jit(solution)/shard_map/all_to_all | solution.py:228
  188.8 81.3 %copy-start.4 = (bf16[128,128]{1,0:T(8,128)(2,1)S(1)}, bf16[128,128]{1,0:T(8,128)(2,1)}, u32[]{:S(2)}) copy-start(bf16[128,128]{1,0:T(8,128)(2,1)} %param.23) | copy-start | bytes 98308
  215.8 52.4 %all-to-all-start.3 = ((bf16[16,2,4,64,128]{4,3,2,1,0:T(8,128)(2,1)}), bf16[16,2,4,64,128]{4,3,2,1,0:T(8,128)(2,1)}, u32[]{:S(2)}, u32[]{:S(2)}) async-start(bf16[16,2,4,64,128]{4,3,2,1,0:T(8,128)(2,1)} %bitcast.117), calls=%async_computation.3 | async-start | bytes 4194304 | tf_op jit(solution)/shard_map/all_to_all | solution.py:228
  268.2 4.3 %copy-start.3 = (bf16[16,512,128]{2,1,0:T(8,128)(2,1)S(1)}, bf16[16,512,128]{2,1,0:T(8,128)(2,1)}, u32[]{:S(2)}) copy-start(bf16[16,512,128]{2,1,0:T(8,128)(2,1)} %copy-done.2) | copy-start | bytes 6291460
  270.1 5.4 %copy-start.1 = (bf16[128,256]{1,0:T(8,128)(2,1)S(1)}, bf16[128,256]{1,0:T(8,128)(2,1)}, u32[]{:S(2)}) copy-start(bf16[128,256]{1,0:T(8,128)(2,1)} %param.13) | copy-start | bytes 196612
where the time goes:
time: 276 us
  waiting for transfers between devices  82.6 us (30%)
  matrix products  62.5 us (23%)
  local copies, waits for them, and re-layouts  48 us (17%)
  Pallas kernels  32 us (12%)
  starting transfers between devices  30.9 us (11%)
  other arithmetic  18.9 us (7%)
    all_to_all x2, waiting for transfers between devices, body(): returned = lax.all_to_all(returned, ('row', 'col'), 0, 0, tiled=True)  65.8 us
    dot_general x2, matrix products, body(): jnp.dot(hidden, project_weight, preferred_element_type=jnp.float32)  47.8 us
    pallas_call x2, Pallas kernels, grid_attention(): pl.pallas_call(attention_kernel, grid=(count // block,), in_specs=[pl.Blo...  32 us
    all_to_all x2, waiting for transfers between devices, body(): moved = lax.all_to_all(pair, ('row', 'col'), 0, 0, tiled=True)  16.8 us
    gather x2, local copies, waits for them, and re-layouts, grid_bias(): return jnp.take(position_bias, offset_index, axis=1)  16.5 us
    dot_general x5, matrix products, expand_layer(): jnp.dot(features, expand_weight, preferred_element_type=jnp.float32)  11.7 us
    transpose x2, local copies, waits for them, and re-layouts, body(): returned = heads_out.reshape(sub, pp, inner_cols, G, col_size, across, ch...  10.8 us
    all_to_all x2, starting transfers between devices, body(): moved = lax.all_to_all(pair, ('row', 'col'), 0, 0, tiled=True)  10.2 us
  transfers between devices with their start and end apart: 8, of which 4 were waited for; matrix products, arithmetic and copies ran while one was open for 33% of the time, Pallas kernels for 12%

commit v1 on v0

--- a/solution.py
+++ b/solution.py
@@ -192,16 +192,20 @@
     across = G // lax.axis_size("col")
     stride = col_count // across
     table = grid_bias(position_bias, G)
-    pieces = 2 if row_count % (2 * row_size) == 0 and (row_count // 2) % G == 0 else 1
-    span = row_count // pieces
+    if row_count % row_size == 0 and row_count > row_size:
+        spans = [row_size, row_count - row_size]
+    else:
+        spans = [row_count]
+    pieces = len(spans)
     col_size = lax.axis_size("col")
     sub = row_size // G
-    pp = span // row_size
     inner_cols = stride // col_size
     source = expanded
     outs = []
     for piece in range(pieces):
-        first = piece * span
+        first = sum(spans[:piece])
+        span = spans[piece]
+        pp = span // row_size
         window = expanded_window(source, edges, first, span)
         hidden = depthwise(window, depth_weight, depth_bias, span, col_count)
         after_conv = (

time: 276 us -> 302 us (1.094)
  waiting for transfers between devices: 82.6 us -> 104 us
    all_to_all x2, waiting for transfers between devices: 16.8 us -> 37.6 us  [body(): moved = lax.all_to_all(pair, ('row', 'col'), 0, 0, tiled=True)]
  transfers between devices with their start and end apart: 8 -> 8, of which waited for: 4 -> 2; matrix products, arithmetic and copies ran while one was open for 33% -> 35% of each run, Pallas kernels for 12% -> 11%
where the time goes in v1:
time: 302 us; the launch traced here: 301 us
  waiting for transfers between devices  104 us (34%)
  matrix products  64.3 us (21%)
  local copies, waits for them, and re-layouts  46.1 us (15%)
  starting transfers between devices  33.9 us (11%)
  Pallas kernels  31.9 us (11%)
  other arithmetic  19.9 us (7%)
    all_to_all x2, waiting for transfers between devices, body(): returned = lax.all_to_all(returned, ('row', 'col'), 0, 0, tiled=True)  66.1 us
    dot_general x2, matrix products, body(): jnp.dot(hidden, project_weight, preferred_element_type=jnp.float32)  49.1 us
    all_to_all x2, waiting for transfers between devices, body(): moved = lax.all_to_all(pair, ('row', 'col'), 0, 0, tiled=True)  37.6 us
    pallas_call x2, Pallas kernels, grid_attention(): pl.pallas_call(attention_kernel, grid=(count // block,), in_specs=[pl.Blo...  31.9 us
    gather x2, local copies, waits for them, and re-layouts, grid_bias(): return jnp.take(position_bias, offset_index, axis=1)  16.5 us
    all_to_all x2, starting transfers between devices, body(): moved = lax.all_to_all(pair, ('row', 'col'), 0, 0, tiled=True)  13.2 us
    dot_general x5, matrix products, expand_layer(): jnp.dot(features, expand_weight, preferred_element_type=jnp.float32)  11.6 us
    all_to_all x2, starting transfers between devices, body(): returned = lax.all_to_all(returned, ('row', 'col'), 0, 0, tiled=True)  11.1 us
  transfers between devices with their start and end apart: 8, of which 2 were waited for; matrix products, arithmetic and copies ran while one was open for 35% of the time, Pallas kernels for 11%

profile of v1, /device:TPU:13, one launch (start us, length us, event | category | flops | bytes accessed | tf_op | source)
XLA Modules:
  0.0 300.6 jit_solution(17952593867539959548)
XLA Ops:
  1.0 3.1 %collective-permute-start = (bf16[512,128]{1,0:T(8,128)(2,1)S(1)}, bf16[512,128]{1,0:T(8,128)(2,1)S(1)}, u32[]{:S(2)}, u32[]{:S(2)}) collective-permute-start(bf16[512,128]{1,0:T(8,128)(2,1)S(1)} %get-tuple-element.11), channel_id=1, source_target_pairs={{0,2},{2,4},{4,6},{6,8},{8,10},{10,12},{12,14},{1,3},{3,5},{5,7},{... | collective-permute-start | bytes 393224 | tf_op jit(solution)/shard_map/ppermute | solution.py:148
  4.2 2.1 collective-permute-start.1
  7.3 10.6 %fusion.7 = bf16[32,512,256]{2,1,0:T(8,128)(2,1)} fusion(bf16[32,512,128]{2,1,0:T(8,128)(2,1)} %param.12, f32[256]{0:T(256)} %param.14, bf16[128,256]{1,0:T(8,128)(2,1)S(1)} %copy-done), kind=kOutput, calls=%fused_computation.10 | convolution fusion | flops 1115684864 | bytes 12649472 | tf_op jit(solution)/shard_map/dot_general | solution.py:30
  18.1 3.1 %collective-permute-start.3 = (bf16[34,128]{1,0:T(8,128)(2,1)S(1)}, bf16[34,128]{1,0:T(8,128)(2,1)S(1)}, u32[]{:S(2)}, u32[]{:S(2)}) collective-permute-start(bf16[34,128]{1,0:T(8,128)(2,1)S(1)} %pad_maximum_fusion.9), channel_id=1, source_target_pairs={{1,0},{3,2},{5,4},{7,6},{9,8},{11,10},{13,12},{15,14},{17,16},{19,... | collective-permute-start | bytes 26120 | tf_op jit(solution)/shard_map/ppermute | solution.py:154
  21.3 1.3 collective-permute-start.2
  23.0 1.9 pad_maximum_fusion.4
  25.9 12.9 %convert_reduce_fusion.1 = (f32[8,512]{1,0:T(8,128)S(1)}, bf16[8,512,128]{2,1,0:T(8,128)(2,1)S(1)}) fusion(f32[128]{0:T(128)S(1)} %copy-done.21, bf16[256,128]{1,0:T(8,128)(2,1)S(1)} %copy-done.16, bf16[10,512,256]{2,1,0:T(8,128)(2,1)S(1)} %pad_maximum_fusion.4, bf16[10,1,256]{2,1,0:T(2,128)(2,1)S(1)} %copy.38, bf16[10,1,256]{2,1,0:T(2,128)(2,1)S(1)} %copy.36, ...), kind=kOutput, calls=%fused_computation.61 | convolution fusion | flops 331345920 | bytes 17666560 | tf_op jit(solution)/shard_map/dot_general | solution.py:213
  38.8 1.3 fusion.44
  40.1 1.3 fusion.47
  42.5 7.0 %all-to-all-start = ((bf16[16,1,4,64,128]{4,3,2,1,0:T(8,128)(2,1)}), bf16[16,1,4,64,128]{4,3,2,1,0:T(8,128)(2,1)}, u32[]{:S(2)}, u32[]{:S(2)}) async-start(bf16[16,1,4,64,128]{4,3,2,1,0:T(8,128)(2,1)} %bitcast.29), calls=%async_computation | async-start | bytes 2097152 | tf_op jit(solution)/shard_map/all_to_all | solution.py:220
  49.6 4.3 %fusion.18 = bf16[26,512,256]{2,1,0:T(8,128)(2,1)S(1)} fusion(bf16[32,512,256]{2,1,0:T(8,128)(2,1)} %fusion.7, bf16[1,512,256]{2,1,0:T(8,128)(2,1)S(1)} %fusion.74), kind=kLoop, calls=%fused_computation.30 | loop fusion | flops 3407872 | bytes 15466496 | tf_op jit(solution)/shard_map/concatenate | solution.py:137
  54.0 36.2 %convert_reduce_fusion = (f32[24,512]{1,0:T(8,128)S(1)}, bf16[24,512,128]{2,1,0:T(8,128)(2,1)S(1)}) fusion(f32[128]{0:T(128)S(1)} %copy-done.22, bf16[256,128]{1,0:T(8,128)(2,1)S(1)} %copy-done.17, bf16[26,1,256]{2,1,0:T(2,128)(2,1)S(1)} %copy.47, bf16[26,1,256]{2,1,0:T(2,128)(2,1)S(1)} %copy.46, bf16[26,512,256]{2,1,0:T(8,128)(2,1)S(1)} %fusion.18, ...), kind=kOutput, calls=%fused_computation.25 | convolution fusion | flops 994037760 | bytes 34492928 | tf_op jit(solution)/shard_map/dot_general | solution.py:213
  90.2 3.6 %fusion.19 = f32[24,512]{1,0:T(8,128)S(1)} fusion(bf16[24,512,128]{2,1,0:T(8,128)(2,1)S(1)} %get-tuple-element.31, f32[24,512]{1,0:T(8,128)S(1)} %broadcast_multiply_fusion), kind=kLoop, calls=%fused_computation.31 | loop fusion | flops 6279168 | bytes 3244032 | tf_op jit(solution)/shard_map/reduce_sum | solution.py:49
  93.9 4.1 %fusion.22 = bf16[24,512,128]{2,1,0:T(8,128)(2,1)S(1)} fusion(bf16[24,512,128]{2,1,0:T(8,128)(2,1)S(1)} %get-tuple-element.31, f32[128]{0:T(128)S(1)} %copy-done.8, f32[128]{0:T(128)S(1)} %copy-done.9, f32[24,512]{1,0:T(8,128)S(1)} %add_rsqrt_fusion, f32[24,512]{1,0:T(8,128)S(1)} %broadcast_multiply_fusion), kind=kLoop, calls=%fused_computation.34 | loop fusion | flops 9437184 | bytes 6390784 | tf_op jit(solution)/shard_map/convert_element_type | solution.py:50
  98.0 2.7 copy.48
  100.7 6.2 %all-to-all-start.2 = ((bf16[16,3,4,64,128]{4,3,2,1,0:T(8,128)(2,1)}), bf16[16,3,4,64,128]{4,3,2,1,0:T(8,128)(2,1)}, u32[]{:S(2)}, u32[]{:S(2)}) async-start(bf16[16,3,4,64,128]{4,3,2,1,0:T(8,128)(2,1)} %bitcast.109), calls=%async_computation.2 | async-start | bytes 6291456 | tf_op jit(solution)/shard_map/all_to_all | solution.py:220
  107.1 14.2 %gather_fusion = f32[4096,4]{1,0:T(8,128)} fusion(f32[4,225]{0,1:T(8,128)S(1)} %copy.42, s32[4096]{0:T(1024)S(1)} %broadcast_clamp_fusion), kind=kCustom, calls=%fused_computation | custom fusion | bytes 147456 | tf_op jit(solution)/shard_map/jit(_take)/gather | solution.py:62
  121.3 2.3 copy.52
  124.4 3.0 %copy.41 = bf16[8,1,2,1,4,64,128]{6,4,2,0,5,3,1:T(4,128)(2,1)} copy(bf16[8,1,2,1,4,64,128]{6,5,4,2,0,3,1:T(8,128)(2,1)} %bitcast.30) | data formatting | bytes 2097152 | tf_op jit(solution)/shard_map/reshape | solution.py:222
  127.4 8.9 %shard_map.118 = bf16[64,64,128]{2,1,0:T(8,128)(2,1)} custom-call(bf16[64,64,128]{2,1,0:T(8,128)(2,1)} %bitcast.117, bf16[128,384]{1,0:T(8,128)(2,1)} %w_ref.3, f32[4,64,64]{2,1,0:T(8,128)} %select_bitcast_fusion.bias_ref), custom_call_target="tpu_custom_call" | custom-call | tf_op jit(solution)/shard_map/pallas_call | solution.py:112
  136.3 2.9 copy.44
  139.2 37.6 %all-to-all-done.2 = bf16[16,3,4,64,128]{4,3,2,1,0:T(8,128)(2,1)} async-done(((bf16[16,3,4,64,128]{4,3,2,1,0:T(8,128)(2,1)}), bf16[16,3,4,64,128]{4,3,2,1,0:T(8,128)(2,1)}, u32[]{:S(2)}, u32[]{:S(2)}) %all-to-all-start.2) | async-done | bytes 3145760 | tf_op jit(solution)/shard_map/all_to_all | solution.py:220
  176.8 4.9 %all-to-all-start.1 = ((bf16[16,1,4,64,128]{4,3,2,1,0:T(8,128)(2,1)}), bf16[16,1,4,64,128]{4,3,2,1,0:T(8,128)(2,1)}, u32[]{:S(2)}, u32[]{:S(2)}) async-start(bf16[16,1,4,64,128]{4,3,2,1,0:T(8,128)(2,1)} %bitcast.116), calls=%async_computation.1 | async-start | bytes 2097152 | tf_op jit(solution)/shard_map/all_to_all | solution.py:232
  181.7 6.0 %copy.49 = bf16[8,1,2,3,4,64,128]{6,4,2,0,5,3,1:T(4,128)(2,1)} copy(bf16[8,1,2,3,4,64,128]{6,5,4,3,2,0,1:T(8,128)(2,1)} %bitcast.48) | data formatting | bytes 6291456 | tf_op jit(solution)/shard_map/reshape | solution.py:222
  187.7 23.0 %shard_map.119 = bf16[192,64,128]{2,1,0:T(8,128)(2,1)} custom-call(bf16[192,64,128]{2,1,0:T(8,128)(2,1)} %bitcast.111, bf16[128,384]{1,0:T(8,128)(2,1)} %w_ref.3, f32[4,64,64]{2,1,0:T(8,128)} %select_bitcast_fusion.bias_ref), custom_call_target="tpu_custom_call" | custom-call | tf_op jit(solution)/shard_map/pallas_call | solution.py:112
  210.7 7.2 %copy.50 = bf16[8,1,2,3,4,64,128]{6,5,4,3,2,0,1:T(8,128)(2,1)} copy(bf16[8,1,2,3,4,64,128]{6,4,2,0,5,3,1:T(4,128)(2,1)} %bitcast.112) | data formatting | bytes 6291456 | tf_op jit(solution)/shard_map/transpose | solution.py:229
  217.9 6.1 %all-to-all-start.3 = ((bf16[16,3,4,64,128]{4,3,2,1,0:T(8,128)(2,1)}), bf16[16,3,4,64,128]{4,3,2,1,0:T(8,128)(2,1)}, u32[]{:S(2)}, u32[]{:S(2)}) async-start(bf16[16,3,4,64,128]{4,3,2,1,0:T(8,128)(2,1)} %bitcast.110), calls=%async_computation.3 | async-start | bytes 6291456 | tf_op jit(solution)/shard_map/all_to_all | solution.py:232
  224.1 1.3 copy.45
  225.4 2.6 fusion.48
  228.0 66.0 %all-to-all-done.3 = bf16[16,3,4,64,128]{4,3,2,1,0:T(8,128)(2,1)} async-done(((bf16[16,3,4,64,128]{4,3,2,1,0:T(8,128)(2,1)}), bf16[16,3,4,64,128]{4,3,2,1,0:T(8,128)(2,1)}, u32[]{:S(2)}, u32[]{:S(2)}) %all-to-all-start.3) | async-done | bytes 3145760 | tf_op jit(solution)/shard_map/all_to_all | solution.py:232
  294.1 2.9 copy.51
  298.2 2.4 pad_maximum_fusion.3
  (88 shorter events, 6.7 us)
Async XLA Ops:
  0.0 7.2 %copy-start = (bf16[128,256]{1,0:T(8,128)(2,1)S(1)}, bf16[128,256]{1,0:T(8,128)(2,1)}, u32[]{:S(2)}) copy-start(bf16[128,256]{1,0:T(8,128)(2,1)} %param.13) | copy-start | bytes 196612
  1.0 17.1 %collective-permute-start = (bf16[512,128]{1,0:T(8,128)(2,1)S(1)}, bf16[512,128]{1,0:T(8,128)(2,1)S(1)}, u32[]{:S(2)}, u32[]{:S(2)}) collective-permute-start(bf16[512,128]{1,0:T(8,128)(2,1)S(1)} %get-tuple-element.11), channel_id=1, source_target_pairs={{0,2},{2,4},{4,6},{6,8},{8,10},{10,12},{12,14},{1,3},{3,5},{5,7},{... | collective-permute-start | bytes 393224 | tf_op jit(solution)/shard_map/ppermute | solution.py:148
  4.2 13.9 %collective-permute-start.1 = (bf16[512,128]{1,0:T(8,128)(2,1)S(1)}, bf16[512,128]{1,0:T(8,128)(2,1)S(1)}, u32[]{:S(2)}, u32[]{:S(2)}) collective-permute-start(bf16[512,128]{1,0:T(8,128)(2,1)S(1)} %get-tuple-element.12), channel_id=1, source_target_pairs={{2,0},{4,2},{6,4},{8,6},{10,8},{12,10},{14,12},{3,1},{5,3},{7,5},{... | collective-permute-start | bytes 393224 | tf_op jit(solution)/shard_map/ppermute | solution.py:149
  7.2 10.7 %copy-start.6 = (f32[3,3,256]{2,1,0:T(4,128)S(1)}, f32[3,3,256]{2,1,0:T(4,128)}, u32[]{:S(2)}) copy-start(f32[3,3,256]{2,1,0:T(4,128)} %param.15) | copy-start | bytes 27652
  7.3 15.4 %copy-start.18 = (f32[256]{0:T(256)S(1)}, f32[256]{0:T(256)}, u32[]{:S(2)}) copy-start(f32[256]{0:T(256)} %param.14) | copy-start | bytes 3076
  17.9 7.8 %copy-start.10 = (f32[1,1,256]{2,1,0:T(1,128)}, f32[1,1,256]{2,1,0:T(1,128)S(1)}, u32[]{:S(2)}) copy-start(f32[1,1,256]{2,1,0:T(1,128)S(1)} %get-tuple-element.23) | copy-start | bytes 3076
  17.9 7.8 %copy-start.12 = (f32[1,1,256]{2,1,0:T(1,128)}, f32[1,1,256]{2,1,0:T(1,128)S(1)}, u32[]{:S(2)}) copy-start(f32[1,1,256]{2,1,0:T(1,128)S(1)} %get-tuple-element.24) | copy-start | bytes 3076
  17.9 7.8 %copy-start.14 = (f32[1,1,256]{2,1,0:T(1,128)}, f32[1,1,256]{2,1,0:T(1,128)S(1)}, u32[]{:S(2)}) copy-start(f32[1,1,256]{2,1,0:T(1,128)S(1)} %get-tuple-element.25) | copy-start | bytes 3076
  18.1 7.1 %collective-permute-start.3 = (bf16[34,128]{1,0:T(8,128)(2,1)S(1)}, bf16[34,128]{1,0:T(8,128)(2,1)S(1)}, u32[]{:S(2)}, u32[]{:S(2)}) collective-permute-start(bf16[34,128]{1,0:T(8,128)(2,1)S(1)} %pad_maximum_fusion.9), channel_id=1, source_target_pairs={{1,0},{3,2},{5,4},{7,6},{9,8},{11,10},{13,12},{15,14},{17,16},{19,... | collective-permute-start | bytes 26120 | tf_op jit(solution)/shard_map/ppermute | solution.py:154
  21.3 4.2 %collective-permute-start.2 = (bf16[34,128]{1,0:T(8,128)(2,1)S(1)}, bf16[34,128]{1,0:T(8,128)(2,1)S(1)}, u32[]{:S(2)}, u32[]{:S(2)}) collective-permute-start(bf16[34,128]{1,0:T(8,128)(2,1)S(1)} %pad_maximum_fusion.8), channel_id=1, source_target_pairs={{0,1},{2,3},{4,5},{6,7},{8,9},{10,11},{12,13},{14,15},{16,17},{18,... | collective-permute-start | bytes 26120 | tf_op jit(solution)/shard_map/ppermute | solution.py:153
  23.0 2.8 copy-start.16
  23.0 2.8 copy-start.19
  23.0 2.8 copy-start.21
  25.8 14.3 %copy-start.8 = (f32[128]{0:T(128)S(1)}, f32[128]{0:T(128)}, u32[]{:S(2)}) copy-start(f32[128]{0:T(128)} %param.20) | copy-start | bytes 1540
  25.8 14.3 %copy-start.9 = (f32[128]{0:T(128)S(1)}, f32[128]{0:T(128)}, u32[]{:S(2)}) copy-start(f32[128]{0:T(128)} %param.19) | copy-start | bytes 1540
  38.8 1.4 copy-start.2
  42.5 58.2 %all-to-all-start = ((bf16[16,1,4,64,128]{4,3,2,1,0:T(8,128)(2,1)}), bf16[16,1,4,64,128]{4,3,2,1,0:T(8,128)(2,1)}, u32[]{:S(2)}, u32[]{:S(2)}) async-start(bf16[16,1,4,64,128]{4,3,2,1,0:T(8,128)(2,1)} %bitcast.29), calls=%async_computation | async-start | bytes 2097152 | tf_op jit(solution)/shard_map/all_to_all | solution.py:220
  49.5 4.4 %copy-start.5 = (bf16[32,512,128]{2,1,0:T(8,128)(2,1)S(1)}, bf16[32,512,128]{2,1,0:T(8,128)(2,1)}, u32[]{:S(2)}) copy-start(bf16[32,512,128]{2,1,0:T(8,128)(2,1)} %param.12) | copy-start | bytes 12582916
  49.5 4.4 %copy-start.11 = (f32[1,1,256]{2,1,0:T(1,128)S(1)}, f32[1,1,256]{2,1,0:T(1,128)}, u32[]{:S(2)}) copy-start(f32[1,1,256]{2,1,0:T(1,128)} %copy-done.10) | copy-start | bytes 3076
  49.5 4.4 %copy-start.13 = (f32[1,1,256]{2,1,0:T(1,128)S(1)}, f32[1,1,256]{2,1,0:T(1,128)}, u32[]{:S(2)}) copy-start(f32[1,1,256]{2,1,0:T(1,128)} %copy-done.12) | copy-start | bytes 3076
  49.5 4.4 %copy-start.15 = (f32[1,1,256]{2,1,0:T(1,128)S(1)}, f32[1,1,256]{2,1,0:T(1,128)}, u32[]{:S(2)}) copy-start(f32[1,1,256]{2,1,0:T(1,128)} %copy-done.14) | copy-start | bytes 3076
  49.5 4.4 %copy-start.17 = (bf16[256,128]{1,0:T(8,128)(2,1)S(1)}, bf16[256,128]{1,0:T(8,128)(2,1)}, u32[]{:S(2)}) copy-start(bf16[256,128]{1,0:T(8,128)(2,1)} %param.17) | copy-start | bytes 196612
  49.6 4.4 %copy-start.20 = (f32[256]{0:T(256)S(1)}, f32[256]{0:T(256)}, u32[]{:S(2)}) copy-start(f32[256]{0:T(256)} %param.16) | copy-start | bytes 3076
  49.6 4.4 %copy-start.22 = (f32[128]{0:T(128)S(1)}, f32[128]{0:T(128)}, u32[]{:S(2)}) copy-start(f32[128]{0:T(128)} %param.18) | copy-start | bytes 1540
  100.7 6.3 %copy-start.7 = (f32[4,225]{1,0:T(4,128)S(1)}, f32[4,225]{1,0:T(4,128)}, u32[]{:S(2)}) copy-start(f32[4,225]{1,0:T(4,128)} %param.22) | copy-start | bytes 10804
  100.7 76.1 %all-to-all-start.2 = ((bf16[16,3,4,64,128]{4,3,2,1,0:T(8,128)(2,1)}), bf16[16,3,4,64,128]{4,3,2,1,0:T(8,128)(2,1)}, u32[]{:S(2)}, u32[]{:S(2)}) async-start(bf16[16,3,4,64,128]{4,3,2,1,0:T(8,128)(2,1)} %bitcast.109), calls=%async_computation.2 | async-start | bytes 6291456 | tf_op jit(solution)/shard_map/all_to_all | solution.py:220
  176.8 41.1 %all-to-all-start.1 = ((bf16[16,1,4,64,128]{4,3,2,1,0:T(8,128)(2,1)}), bf16[16,1,4,64,128]{4,3,2,1,0:T(8,128)(2,1)}, u32[]{:S(2)}, u32[]{:S(2)}) async-start(bf16[16,1,4,64,128]{4,3,2,1,0:T(8,128)(2,1)} %bitcast.116), calls=%async_computation.1 | async-start | bytes 2097152 | tf_op jit(solution)/shard_map/all_to_all | solution.py:232
  217.9 7.5 %copy-start.4 = (bf16[128,128]{1,0:T(8,128)(2,1)S(1)}, bf16[128,128]{1,0:T(8,128)(2,1)}, u32[]{:S(2)}) copy-start(bf16[128,128]{1,0:T(8,128)(2,1)} %param.23) | copy-start | bytes 98308
  217.9 76.1 %all-to-all-start.3 = ((bf16[16,3,4,64,128]{4,3,2,1,0:T(8,128)(2,1)}), bf16[16,3,4,64,128]{4,3,2,1,0:T(8,128)(2,1)}, u32[]{:S(2)}, u32[]{:S(2)}) async-start(bf16[16,3,4,64,128]{4,3,2,1,0:T(8,128)(2,1)} %bitcast.110), calls=%async_computation.3 | async-start | bytes 6291456 | tf_op jit(solution)/shard_map/all_to_all | solution.py:232
  297.0 1.2 copy-start.3
  297.0 3.6 %copy-start.1 = (bf16[128,256]{1,0:T(8,128)(2,1)S(1)}, bf16[128,256]{1,0:T(8,128)(2,1)}, u32[]{:S(2)}) copy-start(bf16[128,256]{1,0:T(8,128)(2,1)} %param.13) | copy-start | bytes 196612

commit v2 on v0

--- a/solution.py
+++ b/solution.py
@@ -231,13 +231,13 @@
             .transpose(0, 2, 3, 1, 4, 5)
             .reshape(span, col_count, channels)
         )
-        outs.append(
-            (
-                after_conv.astype(jnp.float32)
-                + jnp.dot(returned, output_weight, preferred_element_type=jnp.float32)
-            ).astype(jnp.bfloat16)
-        )
-    return jnp.concatenate(outs, axis=0)
+        outs.append((after_conv, returned))
+    after_conv = jnp.concatenate([a for a, _ in outs], axis=0)
+    returned = jnp.concatenate([r for _, r in outs], axis=0)
+    return (
+        after_conv.astype(jnp.float32)
+        + jnp.dot(returned, output_weight, preferred_element_type=jnp.float32)
+    ).astype(jnp.bfloat16)
 
 
 def solution(mesh):

time: 276 us -> 304 us (1.10)
  blocking collectives: 0 us -> 53.2 us
  waiting for transfers between devices: 82.6 us -> 69.9 us
  starting transfers between devices: 30.9 us -> 25.1 us
  other arithmetic: 18.9 us -> 13.9 us
    all_to_all x0 -> x1, blocking collectives: none -> 53.2 us  [body(): moved = lax.all_to_all(pair, ('row', 'col'), 0, 0, tiled=True)]
    all_to_all x2 -> x1, waiting for transfers between devices: 16.8 us -> 4.03 us  [body(): moved = lax.all_to_all(pair, ('row', 'col'), 0, 0, tiled=True)]
    all_to_all x2 -> x1, starting transfers between devices: 10.2 us -> 5.12 us  [body(): moved = lax.all_to_all(pair, ('row', 'col'), 0, 0, tiled=True)]
  transfers between devices with their start and end apart: 8 -> 7, of which waited for: 4 -> 3; matrix products, arithmetic and copies ran while one was open for 33% -> 18% of each run, Pallas kernels for 12% -> 11%
where the time goes in v2:
time: 304 us
  waiting for transfers between devices  69.9 us (23%)
  matrix products  63.5 us (21%)
  blocking collectives  53.2 us (18%)
  local copies, waits for them, and re-layouts  45.5 us (15%)
  Pallas kernels  32 us (11%)
  starting transfers between devices  25.1 us (8%)
  other arithmetic  13.9 us (5%)
    all_to_all x2, waiting for transfers between devices, body(): returned = lax.all_to_all(returned, ('row', 'col'), 0, 0, tiled=True)  65.8 us
    all_to_all x1, blocking collectives, body(): moved = lax.all_to_all(pair, ('row', 'col'), 0, 0, tiled=True)  53.2 us
    dot_general x2, matrix products, body(): jnp.dot(hidden, project_weight, preferred_element_type=jnp.float32)  46.4 us
    pallas_call x2, Pallas kernels, grid_attention(): pl.pallas_call(attention_kernel, grid=(count // block,), in_specs=[pl.Blo...  32 us
    gather x2, local copies, waits for them, and re-layouts, grid_bias(): return jnp.take(position_bias, offset_index, axis=1)  16.5 us
    dot_general x5, matrix products, expand_layer(): jnp.dot(features, expand_weight, preferred_element_type=jnp.float32)  11.7 us
    transpose x2, local copies, waits for them, and re-layouts, body(): returned = heads_out.reshape(sub, pp, inner_cols, G, col_size, across, ch...  10.8 us
    all_to_all x2, starting transfers between devices, body(): returned = lax.all_to_all(returned, ('row', 'col'), 0, 0, tiled=True)  9.82 us
  transfers between devices with their start and end apart: 7, of which 3 were waited for; matrix products, arithmetic and copies ran while one was open for 18% of the time, Pallas kernels for 11%

profile of v2, /device:TPU:13, one launch (start us, length us, event | category | flops | bytes accessed | tf_op | source)
XLA Modules:
  0.0 303.7 jit_solution(5783108587833694468)
XLA Ops:
  0.0 1.0 slice_bitcast_fusion
  1.0 3.1 %collective-permute-start = (bf16[512,128]{1,0:T(8,128)(2,1)S(1)}, bf16[512,128]{1,0:T(8,128)(2,1)S(1)}, u32[]{:S(2)}, u32[]{:S(2)}) collective-permute-start(bf16[512,128]{1,0:T(8,128)(2,1)S(1)} %get-tuple-element.12), channel_id=1, source_target_pairs={{0,2},{2,4},{4,6},{6,8},{8,10},{10,12},{12,14},{1,3},{3,5},{5,7},{... | collective-permute-start | bytes 393224 | tf_op jit(solution)/shard_map/ppermute | solution.py:148
  4.2 2.1 collective-permute-start.1
  7.3 10.7 %fusion.7 = bf16[32,512,256]{2,1,0:T(8,128)(2,1)} fusion(bf16[32,512,128]{2,1,0:T(8,128)(2,1)} %param.12, f32[256]{0:T(256)} %param.14, bf16[128,256]{1,0:T(8,128)(2,1)S(1)} %copy-done), kind=kOutput, calls=%fused_computation.9 | convolution fusion | flops 1115684864 | bytes 12649472 | tf_op jit(solution)/shard_map/dot_general | solution.py:30
  18.1 1.3 collective-permute-start.2
  19.5 3.6 %collective-permute-start.3 = (bf16[34,128]{1,0:T(8,128)(2,1)S(1)}, bf16[34,128]{1,0:T(8,128)(2,1)S(1)}, u32[]{:S(2)}, u32[]{:S(2)}) collective-permute-start(bf16[34,128]{1,0:T(8,128)(2,1)S(1)} %pad_maximum_fusion.7), channel_id=1, source_target_pairs={{1,0},{3,2},{5,4},{7,6},{9,8},{11,10},{13,12},{15,14},{17,16},{19,... | collective-permute-start | bytes 26120 | tf_op jit(solution)/shard_map/ppermute | solution.py:154
  23.5 2.7 fusion.29
  27.0 23.1 %convert_reduce_fusion.1 = (f32[16,512]{1,0:T(8,128)S(1)}, bf16[16,512,128]{2,1,0:T(8,128)(2,1)S(1)}) fusion(f32[128]{0:T(128)S(1)} %copy-done.12, bf16[256,128]{1,0:T(8,128)(2,1)S(1)} %copy-done.8, bf16[18,512,256]{2,1,0:T(8,128)(2,1)S(1)} %fusion.29, bf16[18,1,256]{2,1,0:T(2,128)(2,1)S(1)} %copy.22, bf16[18,1,256]{2,1,0:T(2,128)(2,1)S(1)} %copy.20, ...), kind=kOutput, calls=%fused_computation.44 | convolution fusion | flops 662691840 | bytes 26098176 | tf_op jit(solution)/shard_map/dot_general | solution.py:209
  50.2 2.4 fusion.42
  52.6 2.5 fusion.45
  55.1 1.5 copy.23
  57.1 23.3 %convert_reduce_fusion = (f32[16,512]{1,0:T(8,128)S(1)}, bf16[16,512,128]{2,1,0:T(8,128)(2,1)S(1)}) fusion(f32[128]{0:T(128)S(1)} %copy-done.12, bf16[256,128]{1,0:T(8,128)(2,1)S(1)} %copy-done.8, bf16[18,512,256]{2,1,0:T(8,128)(2,1)S(1)} %fusion.28, bf16[18,1,256]{2,1,0:T(2,128)(2,1)S(1)} %copy.25, bf16[18,1,256]{2,1,0:T(2,128)(2,1)S(1)} %copy.24, ...), kind=kOutput, calls=%fused_computation.42 | convolution fusion | flops 662691840 | bytes 26098176 | tf_op jit(solution)/shard_map/dot_general | solution.py:209
  80.4 2.4 fusion.38
  82.8 2.5 fusion.41
  85.6 53.2 %all_to_all.20 = bf16[16,2,4,64,128]{4,3,2,1,0:T(8,128)(2,1)} all-to-all(bf16[16,2,4,64,128]{4,3,2,1,0:T(8,128)(2,1)S(1)} %bitcast.114), channel_id=1, replica_groups=mesh['groups'=2,'row'=8,'col'=2] {'row','col'}, dimensions={0} | all-to-all | bytes 4194304 | tf_op jit(solution)/shard_map/all_to_all | solution.py:216
  138.8 5.1 %all-to-all-start = ((bf16[16,2,4,64,128]{4,3,2,1,0:T(8,128)(2,1)}), bf16[16,2,4,64,128]{4,3,2,1,0:T(8,128)(2,1)}, u32[]{:S(2)}, u32[]{:S(2)}) async-start(bf16[16,2,4,64,128]{4,3,2,1,0:T(8,128)(2,1)} %bitcast.108), calls=%async_computation | async-start | bytes 4194304 | tf_op jit(solution)/shard_map/all_to_all | solution.py:216
  144.3 14.2 %gather_fusion = f32[4096,4]{1,0:T(8,128)} fusion(f32[4,225]{0,1:T(8,128)S(1)} %copy.27, s32[4096]{0:T(1024)S(1)} %broadcast_clamp_fusion), kind=kCustom, calls=%fused_computation | custom fusion | bytes 147456 | tf_op jit(solution)/shard_map/jit(_take)/gather | solution.py:62
  158.5 2.3 copy.35
  161.5 4.5 %copy.32 = bf16[8,1,2,2,4,64,128]{6,4,2,0,5,3,1:T(4,128)(2,1)} copy(bf16[8,1,2,2,4,64,128]{6,5,4,3,2,0,1:T(8,128)(2,1)} %bitcast.109) | data formatting | bytes 4194304 | tf_op jit(solution)/shard_map/reshape | solution.py:218
  166.1 16.0 %shard_map.119 = bf16[128,64,128]{2,1,0:T(8,128)(2,1)} custom-call(bf16[128,64,128]{2,1,0:T(8,128)(2,1)} %bitcast.115, bf16[128,384]{1,0:T(8,128)(2,1)} %w_ref.3, f32[4,64,64]{2,1,0:T(8,128)} %select_bitcast_fusion.bias_ref), custom_call_target="tpu_custom_call" | custom-call | tf_op jit(solution)/shard_map/pallas_call | solution.py:112
  182.1 5.3 %copy.33 = bf16[8,1,2,2,4,64,128]{6,5,4,3,2,0,1:T(8,128)(2,1)} copy(bf16[8,1,2,2,4,64,128]{6,4,2,0,5,3,1:T(4,128)(2,1)} %bitcast.116) | data formatting | bytes 4194304 | tf_op jit(solution)/shard_map/transpose | solution.py:225
  187.4 4.0 %all-to-all-done = bf16[16,2,4,64,128]{4,3,2,1,0:T(8,128)(2,1)} async-done(((bf16[16,2,4,64,128]{4,3,2,1,0:T(8,128)(2,1)}), bf16[16,2,4,64,128]{4,3,2,1,0:T(8,128)(2,1)}, u32[]{:S(2)}, u32[]{:S(2)}) %all-to-all-start) | async-done | bytes 2097184 | tf_op jit(solution)/shard_map/all_to_all | solution.py:216
  191.5 4.9 %all-to-all-start.3 = ((bf16[16,2,4,64,128]{4,3,2,1,0:T(8,128)(2,1)}), bf16[16,2,4,64,128]{4,3,2,1,0:T(8,128)(2,1)}, u32[]{:S(2)}, u32[]{:S(2)}) async-start(bf16[16,2,4,64,128]{4,3,2,1,0:T(8,128)(2,1)} %bitcast.110), calls=%async_computation.3 | async-start | bytes 4194304 | tf_op jit(solution)/shard_map/all_to_all | solution.py:228
  196.4 4.6 %copy.26 = bf16[8,1,2,2,4,64,128]{6,4,2,0,5,3,1:T(4,128)(2,1)} copy(bf16[8,1,2,2,4,64,128]{6,5,4,3,2,0,1:T(8,128)(2,1)} %bitcast.32) | data formatting | bytes 4194304 | tf_op jit(solution)/shard_map/reshape | solution.py:218
  201.0 16.0 %shard_map.118 = bf16[128,64,128]{2,1,0:T(8,128)(2,1)} custom-call(bf16[128,64,128]{2,1,0:T(8,128)(2,1)} %bitcast.112, bf16[128,384]{1,0:T(8,128)(2,1)} %w_ref.3, f32[4,64,64]{2,1,0:T(8,128)} %select_bitcast_fusion.bias_ref), custom_call_target="tpu_custom_call" | custom-call | tf_op jit(solution)/shard_map/pallas_call | solution.py:112
  217.0 5.4 %copy.29 = bf16[8,1,2,2,4,64,128]{6,5,4,3,2,0,1:T(8,128)(2,1)} copy(bf16[8,1,2,2,4,64,128]{6,4,2,0,5,3,1:T(4,128)(2,1)} %bitcast.113) | data formatting | bytes 4194304 | tf_op jit(solution)/shard_map/transpose | solution.py:225
  222.4 21.5 %all-to-all-done.3 = bf16[16,2,4,64,128]{4,3,2,1,0:T(8,128)(2,1)} async-done(((bf16[16,2,4,64,128]{4,3,2,1,0:T(8,128)(2,1)}), bf16[16,2,4,64,128]{4,3,2,1,0:T(8,128)(2,1)}, u32[]{:S(2)}, u32[]{:S(2)}) %all-to-all-start.3) | async-done | bytes 2097184 | tf_op jit(solution)/shard_map/all_to_all | solution.py:228
  243.9 4.9 %all-to-all-start.1 = ((bf16[16,2,4,64,128]{4,3,2,1,0:T(8,128)(2,1)}), bf16[16,2,4,64,128]{4,3,2,1,0:T(8,128)(2,1)}, u32[]{:S(2)}, u32[]{:S(2)}) async-start(bf16[16,2,4,64,128]{4,3,2,1,0:T(8,128)(2,1)} %bitcast.111), calls=%async_computation.1 | async-start | bytes 4194304 | tf_op jit(solution)/shard_map/all_to_all | solution.py:228
  248.8 3.2 %copy.34 = bf16[8,2,4,2,64,128]{5,4,3,2,1,0:T(8,128)(2,1)} copy(bf16[8,2,4,2,64,128]{5,4,2,1,3,0:T(8,128)(2,1)} %bitcast.53) | data formatting | bytes 4194304 | tf_op jit(solution)/shard_map/transpose | solution.py:231
  252.0 44.3 %all-to-all-done.1 = bf16[16,2,4,64,128]{4,3,2,1,0:T(8,128)(2,1)} async-done(((bf16[16,2,4,64,128]{4,3,2,1,0:T(8,128)(2,1)}), bf16[16,2,4,64,128]{4,3,2,1,0:T(8,128)(2,1)}, u32[]{:S(2)}, u32[]{:S(2)}) %all-to-all-start.1) | async-done | bytes 2097184 | tf_op jit(solution)/shard_map/all_to_all | solution.py:228
  296.3 1.9 copy.30
  298.2 5.5 %add_convert_fusion = bf16[32,512,128]{2,1,0:T(8,128)(2,1)} fusion(bf16[16,512,128]{2,1,0:T(8,128)(2,1)} %copy-done.2, bf16[16,512,128]{2,1,0:T(8,128)(2,1)S(1)} %get-tuple-element.33, bf16[16,512,128]{2,1,0:T(8,128)(2,1)} %bitcast.118, bf16[16,512,128]{2,1,0:T(8,128)(2,1)S(1)} %bitcast.119, bf16[128,128]{1,0:T(8,128)(2,1)S(1)} %copy-done.9), kind=kOutput, calls=%fused_computation.32 | convolution fusion | flops 547356672 | bytes 12615680 | tf_op jit(solution)/shard_map/dot_general | solution.py:239
  (68 shorter events, 4.0 us)
Async XLA Ops:
  0.0 7.2 %copy-start = (bf16[128,256]{1,0:T(8,128)(2,1)S(1)}, bf16[128,256]{1,0:T(8,128)(2,1)}, u32[]{:S(2)}) copy-start(bf16[128,256]{1,0:T(8,128)(2,1)} %param.13) | copy-start | bytes 196612
  1.0 17.1 %collective-permute-start = (bf16[512,128]{1,0:T(8,128)(2,1)S(1)}, bf16[512,128]{1,0:T(8,128)(2,1)S(1)}, u32[]{:S(2)}, u32[]{:S(2)}) collective-permute-start(bf16[512,128]{1,0:T(8,128)(2,1)S(1)} %get-tuple-element.12), channel_id=1, source_target_pairs={{0,2},{2,4},{4,6},{6,8},{8,10},{10,12},{12,14},{1,3},{3,5},{5,7},{... | collective-permute-start | bytes 393224 | tf_op jit(solution)/shard_map/ppermute | solution.py:148
  4.2 13.9 %collective-permute-start.1 = (bf16[512,128]{1,0:T(8,128)(2,1)S(1)}, bf16[512,128]{1,0:T(8,128)(2,1)S(1)}, u32[]{:S(2)}, u32[]{:S(2)}) collective-permute-start(bf16[512,128]{1,0:T(8,128)(2,1)S(1)} %get-tuple-element.11), channel_id=1, source_target_pairs={{2,0},{4,2},{6,4},{8,6},{10,8},{12,10},{14,12},{3,1},{5,3},{7,5},{... | collective-permute-start | bytes 393224 | tf_op jit(solution)/shard_map/ppermute | solution.py:149
  7.2 10.7 %copy-start.4 = (f32[3,3,256]{2,1,0:T(4,128)S(1)}, f32[3,3,256]{2,1,0:T(4,128)}, u32[]{:S(2)}) copy-start(f32[3,3,256]{2,1,0:T(4,128)} %param.15) | copy-start | bytes 27652
  7.3 15.8 %copy-start.10 = (f32[256]{0:T(256)S(1)}, f32[256]{0:T(256)}, u32[]{:S(2)}) copy-start(f32[256]{0:T(256)} %param.14) | copy-start | bytes 3076
  18.1 8.4 %collective-permute-start.2 = (bf16[34,128]{1,0:T(8,128)(2,1)S(1)}, bf16[34,128]{1,0:T(8,128)(2,1)S(1)}, u32[]{:S(2)}, u32[]{:S(2)}) collective-permute-start(bf16[34,128]{1,0:T(8,128)(2,1)S(1)} %pad_maximum_fusion.6), channel_id=1, source_target_pairs={{0,1},{2,3},{4,5},{6,7},{8,9},{10,11},{12,13},{14,15},{16,17},{18,... | collective-permute-start | bytes 26120 | tf_op jit(solution)/shard_map/ppermute | solution.py:153
  19.4 7.5 %slice-start = ((s8[8388608]{0:T(1024)(128)(4,1)}), s8[4194304]{0:T(1024)(128)(4,1)S(1)}, s32[]{:S(2)}) async-start(s8[8388608]{0:T(1024)(128)(4,1)} %bitcast.104), calls=%async_computation.4 | async-start | bytes 8388608
  19.5 7.5 %copy-start.3 = (bf16[32,512,128]{2,1,0:T(8,128)(2,1)S(1)}, bf16[32,512,128]{2,1,0:T(8,128)(2,1)}, u32[]{:S(2)}) copy-start(bf16[32,512,128]{2,1,0:T(8,128)(2,1)} %param.12) | copy-start | bytes 12582916
  19.5 7.5 %copy-start.8 = (bf16[256,128]{1,0:T(8,128)(2,1)S(1)}, bf16[256,128]{1,0:T(8,128)(2,1)}, u32[]{:S(2)}) copy-start(bf16[256,128]{1,0:T(8,128)(2,1)} %param.17) | copy-start | bytes 196612
  19.5 7.5 %copy-start.11 = (f32[256]{0:T(256)S(1)}, f32[256]{0:T(256)}, u32[]{:S(2)}) copy-start(f32[256]{0:T(256)} %param.16) | copy-start | bytes 3076
  19.5 7.5 %copy-start.12 = (f32[128]{0:T(128)S(1)}, f32[128]{0:T(128)}, u32[]{:S(2)}) copy-start(f32[128]{0:T(128)} %param.18) | copy-start | bytes 1540
  19.5 7.2 %collective-permute-start.3 = (bf16[34,128]{1,0:T(8,128)(2,1)S(1)}, bf16[34,128]{1,0:T(8,128)(2,1)S(1)}, u32[]{:S(2)}, u32[]{:S(2)}) collective-permute-start(bf16[34,128]{1,0:T(8,128)(2,1)S(1)} %pad_maximum_fusion.7), channel_id=1, source_target_pairs={{1,0},{3,2},{5,4},{7,6},{9,8},{11,10},{13,12},{15,14},{17,16},{19,... | collective-permute-start | bytes 26120 | tf_op jit(solution)/shard_map/ppermute | solution.py:154
  23.5 3.5 %slice-start.1 = ((s8[8388608]{0:T(1024)(128)(4,1)}), s8[4194304]{0:T(1024)(128)(4,1)S(1)}, s32[]{:S(2)}) async-start(s8[8388608]{0:T(1024)(128)(4,1)} %bitcast.104), calls=%async_computation.5 | async-start | bytes 8388608
  27.0 25.6 %copy-start.6 = (f32[128]{0:T(128)S(1)}, f32[128]{0:T(128)}, u32[]{:S(2)}) copy-start(f32[128]{0:T(128)} %param.20) | copy-start | bytes 1540
  27.0 25.6 %copy-start.7 = (f32[128]{0:T(128)S(1)}, f32[128]{0:T(128)}, u32[]{:S(2)}) copy-start(f32[128]{0:T(128)} %param.19) | copy-start | bytes 1540
  80.4 2.4 copy-start.2
  82.8 61.3 %copy-start.5 = (f32[4,225]{1,0:T(4,128)S(1)}, f32[4,225]{1,0:T(4,128)}, u32[]{:S(2)}) copy-start(f32[4,225]{1,0:T(4,128)} %param.22) | copy-start | bytes 10804
  138.8 52.6 %all-to-all-start = ((bf16[16,2,4,64,128]{4,3,2,1,0:T(8,128)(2,1)}), bf16[16,2,4,64,128]{4,3,2,1,0:T(8,128)(2,1)}, u32[]{:S(2)}, u32[]{:S(2)}) async-start(bf16[16,2,4,64,128]{4,3,2,1,0:T(8,128)(2,1)} %bitcast.108), calls=%async_computation | async-start | bytes 4194304 | tf_op jit(solution)/shard_map/all_to_all | solution.py:216
  191.5 52.4 %all-to-all-start.3 = ((bf16[16,2,4,64,128]{4,3,2,1,0:T(8,128)(2,1)}), bf16[16,2,4,64,128]{4,3,2,1,0:T(8,128)(2,1)}, u32[]{:S(2)}, u32[]{:S(2)}) async-start(bf16[16,2,4,64,128]{4,3,2,1,0:T(8,128)(2,1)} %bitcast.110), calls=%async_computation.3 | async-start | bytes 4194304 | tf_op jit(solution)/shard_map/all_to_all | solution.py:228
  217.0 81.2 %copy-start.9 = (bf16[128,128]{1,0:T(8,128)(2,1)S(1)}, bf16[128,128]{1,0:T(8,128)(2,1)}, u32[]{:S(2)}) copy-start(bf16[128,128]{1,0:T(8,128)(2,1)} %param.23) | copy-start | bytes 98308
  243.9 52.4 %all-to-all-start.1 = ((bf16[16,2,4,64,128]{4,3,2,1,0:T(8,128)(2,1)}), bf16[16,2,4,64,128]{4,3,2,1,0:T(8,128)(2,1)}, u32[]{:S(2)}, u32[]{:S(2)}) async-start(bf16[16,2,4,64,128]{4,3,2,1,0:T(8,128)(2,1)} %bitcast.111), calls=%async_computation.1 | async-start | bytes 4194304 | tf_op jit(solution)/shard_map/all_to_all | solution.py:228
  296.3 7.4 %copy-start.1 = (bf16[128,256]{1,0:T(8,128)(2,1)S(1)}, bf16[128,256]{1,0:T(8,128)(2,1)}, u32[]{:S(2)}) copy-start(bf16[128,256]{1,0:T(8,128)(2,1)} %param.13) | copy-start | bytes 196612

commit v3 on v0

--- a/solution.py
+++ b/solution.py
@@ -53,13 +53,17 @@
 
 
 def grid_bias(position_bias, grid_side):
-    position = jnp.arange(grid_side * grid_side, dtype=jnp.int32)
-    row_of = position // grid_side
-    col_of = position % grid_side
-    offset_index = (row_of[:, None] - row_of[None, :] + grid_side - 1) * (2 * grid_side - 1) + (
-        col_of[:, None] - col_of[None, :] + grid_side - 1
-    )
-    return jnp.take(position_bias, offset_index, axis=1)
+    span = 2 * grid_side - 1
+    place = jnp.arange(grid_side, dtype=jnp.int32)
+    offset = (place[:, None] - place[None, :] + grid_side - 1).reshape(-1)
+    pick = (offset[:, None] == jnp.arange(span, dtype=jnp.int32)[None, :]).astype(jnp.float32)
+    grid = position_bias.reshape(-1, span, span)
+    table = jnp.einsum("xa,hab,yb->hxy", pick, grid, pick, precision=lax.Precision.HIGHEST)
+    return (
+        table.reshape(-1, grid_side, grid_side, grid_side, grid_side)
+        .transpose(0, 1, 3, 2, 4)
+        .reshape(-1, grid_side * grid_side, grid_side * grid_side)
+    )
 
 
 def attend(projected, table, head_count):

time: 276 us -> 276 us (level)
  waiting for transfers between devices: 82.6 us -> 95.8 us
  local copies, waits for them, and re-layouts: 48 us -> 35.2 us
    gather x2 -> x0, local copies, waits for them, and re-layouts: 16.5 us -> none  [grid_bias(): return jnp.take(position_bias, offset_index, axis=1)]
    all_to_all x2, waiting for transfers between devices: 16.8 us -> 29.9 us  [body(): moved = lax.all_to_all(pair, ('row', 'col'), 0, 0, tiled=True)]
    reshape x0 -> x4, local copies, waits for them, and re-layouts: none -> 3.77 us  [the longest x1 2.17 us: grid_bias(): return table.reshape(-1, grid_side, grid_side, grid_side, grid_side).tran...]
  transfers between devices with their start and end apart: 8 -> 8, of which waited for: 4 -> 4; matrix products, arithmetic and copies ran while one was open for 33% -> 28% of each run, Pallas kernels for 12% -> 12%
where the time goes in v3:
time: 276 us
  waiting for transfers between devices  95.8 us (35%)
  matrix products  63 us (23%)
  local copies, waits for them, and re-layouts  35.2 us (13%)
  Pallas kernels  32 us (12%)
  starting transfers between devices  30.9 us (11%)
  other arithmetic  18 us (7%)
    all_to_all x2, waiting for transfers between devices, body(): returned = lax.all_to_all(returned, ('row', 'col'), 0, 0, tiled=True)  65.8 us
    dot_general x2, matrix products, body(): jnp.dot(hidden, project_weight, preferred_element_type=jnp.float32)  47.8 us
    pallas_call x2, Pallas kernels, grid_attention(): pl.pallas_call(attention_kernel, grid=(count // block,), in_specs=[pl.Blo...  32 us
    all_to_all x2, waiting for transfers between devices, body(): moved = lax.all_to_all(pair, ('row', 'col'), 0, 0, tiled=True)  29.9 us
    dot_general x5, matrix products, expand_layer(): jnp.dot(features, expand_weight, preferred_element_type=jnp.float32)  11.7 us
    transpose x2, local copies, waits for them, and re-layouts, body(): returned = heads_out.reshape(sub, pp, inner_cols, G, col_size, across, ch...  10.8 us
    all_to_all x2, starting transfers between devices, body(): moved = lax.all_to_all(pair, ('row', 'col'), 0, 0, tiled=True)  10.2 us
    all_to_all x2, starting transfers between devices, body(): returned = lax.all_to_all(returned, ('row', 'col'), 0, 0, tiled=True)  9.82 us
  transfers between devices with their start and end apart: 8, of which 4 were waited for; matrix products, arithmetic and copies ran while one was open for 28% of the time, Pallas kernels for 12%

profile of v3, /device:TPU:13, one launch (start us, length us, event | category | flops | bytes accessed | tf_op | source)
XLA Modules:
  0.0 275.5 jit_solution(14731576253959565066)
XLA Ops:
  1.0 2.1 collective-permute-start.1
  3.2 4.0 %collective-permute-start = (bf16[512,128]{1,0:T(8,128)(2,1)S(1)}, bf16[512,128]{1,0:T(8,128)(2,1)S(1)}, u32[]{:S(2)}, u32[]{:S(2)}) collective-permute-start(bf16[512,128]{1,0:T(8,128)(2,1)S(1)} %get-tuple-element.12), channel_id=1, source_target_pairs={{0,2},{2,4},{4,6},{6,8},{8,10},{10,12},{12,14},{1,3},{3,5},{5,7},{... | collective-permute-start | bytes 393224 | tf_op jit(solution)/shard_map/ppermute | solution.py:152
  8.2 10.7 %fusion.7 = bf16[32,512,256]{2,1,0:T(8,128)(2,1)} fusion(bf16[32,512,128]{2,1,0:T(8,128)(2,1)} %param.12, f32[256]{0:T(256)} %param.14, bf16[128,256]{1,0:T(8,128)(2,1)S(1)} %copy-done), kind=kOutput, calls=%fused_computation.8 | convolution fusion | flops 1115684864 | bytes 12649472 | tf_op jit(solution)/shard_map/dot_general | solution.py:30
  19.0 3.1 %collective-permute-start.3 = (bf16[34,128]{1,0:T(8,128)(2,1)S(1)}, bf16[34,128]{1,0:T(8,128)(2,1)S(1)}, u32[]{:S(2)}, u32[]{:S(2)}) collective-permute-start(bf16[34,128]{1,0:T(8,128)(2,1)S(1)} %pad_maximum_fusion.8), channel_id=1, source_target_pairs={{1,0},{3,2},{5,4},{7,6},{9,8},{11,10},{13,12},{15,14},{17,16},{19,... | collective-permute-start | bytes 26120 | tf_op jit(solution)/shard_map/ppermute | solution.py:158
  22.2 1.6 collective-permute-start.2
  24.2 3.1 %fusion.29 = bf16[18,512,256]{2,1,0:T(8,128)(2,1)S(1)} fusion(bf16[1,512,256]{2,1,0:T(8,128)(2,1)S(1)} %fusion.65, bf16[32,512,256]{2,1,0:T(8,128)(2,1)} %fusion.7), kind=kLoop, calls=%fused_computation.50 | loop fusion | flops 2359296 | bytes 13369344 | tf_op jit(solution)/shard_map/concatenate | solution.py:141
  28.4 23.1 %convert_reduce_fusion.1 = (f32[16,512]{1,0:T(8,128)S(1)}, bf16[16,512,128]{2,1,0:T(8,128)(2,1)S(1)}) fusion(f32[128]{0:T(128)S(1)} %copy-done.14, bf16[256,128]{1,0:T(8,128)(2,1)S(1)} %copy-done.11, bf16[18,512,256]{2,1,0:T(8,128)(2,1)S(1)} %fusion.29, bf16[18,1,256]{2,1,0:T(2,128)(2,1)S(1)} %copy.21, bf16[18,1,256]{2,1,0:T(2,128)(2,1)S(1)} %copy.19, ...), kind=kOutput, calls=%fused_computation.44 | convolution fusion | flops 662691840 | bytes 26098176 | tf_op jit(solution)/shard_map/dot_general | solution.py:213
  51.6 2.4 fusion.42
  54.0 2.5 fusion.45
  58.0 5.3 %all-to-all-start = ((bf16[16,2,4,64,128]{4,3,2,1,0:T(8,128)(2,1)}), bf16[16,2,4,64,128]{4,3,2,1,0:T(8,128)(2,1)}, u32[]{:S(2)}, u32[]{:S(2)}) async-start(bf16[16,2,4,64,128]{4,3,2,1,0:T(8,128)(2,1)} %bitcast.122), calls=%async_computation | async-start | bytes 4194304 | tf_op jit(solution)/shard_map/all_to_all | solution.py:220
  63.4 2.7 fusion.28
  66.9 24.7 %convert_reduce_fusion = (f32[16,512]{1,0:T(8,128)S(1)}, bf16[16,512,128]{2,1,0:T(8,128)(2,1)S(1)}) fusion(f32[128]{0:T(128)S(1)} %copy-done.14, bf16[256,128]{1,0:T(8,128)(2,1)S(1)} %copy-done.11, bf16[18,512,256]{2,1,0:T(8,128)(2,1)S(1)} %fusion.28, bf16[18,1,256]{2,1,0:T(2,128)(2,1)S(1)} %copy.28, bf16[18,1,256]{2,1,0:T(2,128)(2,1)S(1)} %copy.27, ...), kind=kOutput, calls=%fused_computation.41 | convolution fusion | flops 662691840 | bytes 26079744 | tf_op jit(solution)/shard_map/dot_general | solution.py:213
  91.7 2.4 fusion.38
  94.1 2.5 fusion.41
  98.1 12.8 %all-to-all-done = bf16[16,2,4,64,128]{4,3,2,1,0:T(8,128)(2,1)} async-done(((bf16[16,2,4,64,128]{4,3,2,1,0:T(8,128)(2,1)}), bf16[16,2,4,64,128]{4,3,2,1,0:T(8,128)(2,1)}, u32[]{:S(2)}, u32[]{:S(2)}) %all-to-all-start) | async-done | bytes 2097184 | tf_op jit(solution)/shard_map/all_to_all | solution.py:220
  110.9 4.9 %all-to-all-start.2 = ((bf16[16,2,4,64,128]{4,3,2,1,0:T(8,128)(2,1)}), bf16[16,2,4,64,128]{4,3,2,1,0:T(8,128)(2,1)}, u32[]{:S(2)}, u32[]{:S(2)}) async-start(bf16[16,2,4,64,128]{4,3,2,1,0:T(8,128)(2,1)} %bitcast.123), calls=%async_computation.2 | async-start | bytes 4194304 | tf_op jit(solution)/shard_map/all_to_all | solution.py:220
  118.0 2.2 reshape.227.bias_ref
  120.2 4.6 %copy.23 = bf16[8,1,2,2,4,64,128]{6,4,2,0,5,3,1:T(4,128)(2,1)} copy(bf16[8,1,2,2,4,64,128]{6,5,4,3,2,0,1:T(8,128)(2,1)} %bitcast.29) | data formatting | bytes 4194304 | tf_op jit(solution)/shard_map/reshape | solution.py:222
  124.8 16.0 %shard_map.118 = bf16[128,64,128]{2,1,0:T(8,128)(2,1)} custom-call(bf16[128,64,128]{2,1,0:T(8,128)(2,1)} %bitcast.128, bf16[128,384]{1,0:T(8,128)(2,1)} %w_ref.3, f32[4,64,64]{2,1,0:T(8,128)} %reshape.227.bias_ref), custom_call_target="tpu_custom_call" | custom-call | tf_op jit(solution)/shard_map/pallas_call | solution.py:116
  140.8 5.4 %copy.25 = bf16[8,1,2,2,4,64,128]{6,5,4,3,2,0,1:T(8,128)(2,1)} copy(bf16[8,1,2,2,4,64,128]{6,4,2,0,5,3,1:T(4,128)(2,1)} %bitcast.129) | data formatting | bytes 4194304 | tf_op jit(solution)/shard_map/transpose | solution.py:229
  146.2 17.1 %all-to-all-done.2 = bf16[16,2,4,64,128]{4,3,2,1,0:T(8,128)(2,1)} async-done(((bf16[16,2,4,64,128]{4,3,2,1,0:T(8,128)(2,1)}), bf16[16,2,4,64,128]{4,3,2,1,0:T(8,128)(2,1)}, u32[]{:S(2)}, u32[]{:S(2)}) %all-to-all-start.2) | async-done | bytes 2097184 | tf_op jit(solution)/shard_map/all_to_all | solution.py:220
  163.3 4.9 %all-to-all-start.1 = ((bf16[16,2,4,64,128]{4,3,2,1,0:T(8,128)(2,1)}), bf16[16,2,4,64,128]{4,3,2,1,0:T(8,128)(2,1)}, u32[]{:S(2)}, u32[]{:S(2)}) async-start(bf16[16,2,4,64,128]{4,3,2,1,0:T(8,128)(2,1)} %bitcast.124), calls=%async_computation.1 | async-start | bytes 4194304 | tf_op jit(solution)/shard_map/all_to_all | solution.py:232
  168.2 4.6 %copy.30 = bf16[8,1,2,2,4,64,128]{6,4,2,0,5,3,1:T(4,128)(2,1)} copy(bf16[8,1,2,2,4,64,128]{6,5,4,3,2,0,1:T(8,128)(2,1)} %bitcast.48) | data formatting | bytes 4194304 | tf_op jit(solution)/shard_map/reshape | solution.py:222
  172.8 16.0 %shard_map.119 = bf16[128,64,128]{2,1,0:T(8,128)(2,1)} custom-call(bf16[128,64,128]{2,1,0:T(8,128)(2,1)} %bitcast.126, bf16[128,384]{1,0:T(8,128)(2,1)} %w_ref.3, f32[4,64,64]{2,1,0:T(8,128)} %reshape.227.bias_ref), custom_call_target="tpu_custom_call" | custom-call | tf_op jit(solution)/shard_map/pallas_call | solution.py:116
  188.9 5.4 %copy.31 = bf16[8,1,2,2,4,64,128]{6,5,4,3,2,0,1:T(8,128)(2,1)} copy(bf16[8,1,2,2,4,64,128]{6,4,2,0,5,3,1:T(4,128)(2,1)} %bitcast.127) | data formatting | bytes 4194304 | tf_op jit(solution)/shard_map/transpose | solution.py:229
  194.2 21.5 %all-to-all-done.1 = bf16[16,2,4,64,128]{4,3,2,1,0:T(8,128)(2,1)} async-done(((bf16[16,2,4,64,128]{4,3,2,1,0:T(8,128)(2,1)}), bf16[16,2,4,64,128]{4,3,2,1,0:T(8,128)(2,1)}, u32[]{:S(2)}, u32[]{:S(2)}) %all-to-all-start.1) | async-done | bytes 2097184 | tf_op jit(solution)/shard_map/all_to_all | solution.py:232
  215.8 4.9 %all-to-all-start.3 = ((bf16[16,2,4,64,128]{4,3,2,1,0:T(8,128)(2,1)}), bf16[16,2,4,64,128]{4,3,2,1,0:T(8,128)(2,1)}, u32[]{:S(2)}, u32[]{:S(2)}) async-start(bf16[16,2,4,64,128]{4,3,2,1,0:T(8,128)(2,1)} %bitcast.125), calls=%async_computation.3 | async-start | bytes 4194304 | tf_op jit(solution)/shard_map/all_to_all | solution.py:232
  220.7 3.3 %copy.26 = bf16[8,2,4,2,64,128]{5,4,3,2,1,0:T(8,128)(2,1)} copy(bf16[8,2,4,2,64,128]{5,4,2,1,3,0:T(8,128)(2,1)} %bitcast.39) | data formatting | bytes 4194304 | tf_op jit(solution)/shard_map/transpose | solution.py:235
  223.9 44.3 %all-to-all-done.3 = bf16[16,2,4,64,128]{4,3,2,1,0:T(8,128)(2,1)} async-done(((bf16[16,2,4,64,128]{4,3,2,1,0:T(8,128)(2,1)}), bf16[16,2,4,64,128]{4,3,2,1,0:T(8,128)(2,1)}, u32[]{:S(2)}, u32[]{:S(2)}) %all-to-all-start.3) | async-done | bytes 2097184 | tf_op jit(solution)/shard_map/all_to_all | solution.py:232
  268.2 1.9 copy.32
  270.1 2.3 fusion.46
  273.2 2.4 pad_maximum_fusion.6
  (74 shorter events, 10.3 us)
Async XLA Ops:
  0.0 8.1 %copy-start = (bf16[128,256]{1,0:T(8,128)(2,1)S(1)}, bf16[128,256]{1,0:T(8,128)(2,1)}, u32[]{:S(2)}) copy-start(bf16[128,256]{1,0:T(8,128)(2,1)} %param.13) | copy-start | bytes 196612
  1.0 17.9 %collective-permute-start.1 = (bf16[512,128]{1,0:T(8,128)(2,1)S(1)}, bf16[512,128]{1,0:T(8,128)(2,1)S(1)}, u32[]{:S(2)}, u32[]{:S(2)}) collective-permute-start(bf16[512,128]{1,0:T(8,128)(2,1)S(1)} %get-tuple-element.11), channel_id=1, source_target_pairs={{2,0},{4,2},{6,4},{8,6},{10,8},{12,10},{14,12},{3,1},{5,3},{7,5},{... | collective-permute-start | bytes 393224 | tf_op jit(solution)/shard_map/ppermute | solution.py:153
  3.2 15.8 %collective-permute-start = (bf16[512,128]{1,0:T(8,128)(2,1)S(1)}, bf16[512,128]{1,0:T(8,128)(2,1)S(1)}, u32[]{:S(2)}, u32[]{:S(2)}) collective-permute-start(bf16[512,128]{1,0:T(8,128)(2,1)S(1)} %get-tuple-element.12), channel_id=1, source_target_pairs={{0,2},{2,4},{4,6},{6,8},{8,10},{10,12},{12,14},{1,3},{3,5},{5,7},{... | collective-permute-start | bytes 393224 | tf_op jit(solution)/shard_map/ppermute | solution.py:152
  8.1 10.7 %copy-start.7 = (f32[3,3,256]{2,1,0:T(4,128)S(1)}, f32[3,3,256]{2,1,0:T(4,128)}, u32[]{:S(2)}) copy-start(f32[3,3,256]{2,1,0:T(4,128)} %param.15) | copy-start | bytes 27652
  8.2 15.7 %copy-start.12 = (f32[256]{0:T(256)S(1)}, f32[256]{0:T(256)}, u32[]{:S(2)}) copy-start(f32[256]{0:T(256)} %param.14) | copy-start | bytes 3076
  19.0 8.6 %collective-permute-start.3 = (bf16[34,128]{1,0:T(8,128)(2,1)S(1)}, bf16[34,128]{1,0:T(8,128)(2,1)S(1)}, u32[]{:S(2)}, u32[]{:S(2)}) collective-permute-start(bf16[34,128]{1,0:T(8,128)(2,1)S(1)} %pad_maximum_fusion.8), channel_id=1, source_target_pairs={{1,0},{3,2},{5,4},{7,6},{9,8},{11,10},{13,12},{15,14},{17,16},{19,... | collective-permute-start | bytes 26120 | tf_op jit(solution)/shard_map/ppermute | solution.py:158
  22.2 5.9 %slice-start = ((s8[8388608]{0:T(1024)(128)(4,1)}), s8[4194304]{0:T(1024)(128)(4,1)S(1)}, s32[]{:S(2)}) async-start(s8[8388608]{0:T(1024)(128)(4,1)} %bitcast.116), calls=%async_computation.4 | async-start | bytes 8388608
  22.2 5.9 %copy-start.5 = (bf16[32,512,128]{2,1,0:T(8,128)(2,1)S(1)}, bf16[32,512,128]{2,1,0:T(8,128)(2,1)}, u32[]{:S(2)}) copy-start(bf16[32,512,128]{2,1,0:T(8,128)(2,1)} %param.12) | copy-start | bytes 12582916
  22.2 5.9 %copy-start.11 = (bf16[256,128]{1,0:T(8,128)(2,1)S(1)}, bf16[256,128]{1,0:T(8,128)(2,1)}, u32[]{:S(2)}) copy-start(bf16[256,128]{1,0:T(8,128)(2,1)} %param.17) | copy-start | bytes 196612
  22.2 5.9 %copy-start.13 = (f32[256]{0:T(256)S(1)}, f32[256]{0:T(256)}, u32[]{:S(2)}) copy-start(f32[256]{0:T(256)} %param.16) | copy-start | bytes 3076
  22.2 5.9 %copy-start.14 = (f32[128]{0:T(128)S(1)}, f32[128]{0:T(128)}, u32[]{:S(2)}) copy-start(f32[128]{0:T(128)} %param.18) | copy-start | bytes 1540
  22.2 5.6 %collective-permute-start.2 = (bf16[34,128]{1,0:T(8,128)(2,1)S(1)}, bf16[34,128]{1,0:T(8,128)(2,1)S(1)}, u32[]{:S(2)}, u32[]{:S(2)}) collective-permute-start(bf16[34,128]{1,0:T(8,128)(2,1)S(1)} %pad_maximum_fusion.7), channel_id=1, source_target_pairs={{0,1},{2,3},{4,5},{6,7},{8,9},{10,11},{12,13},{14,15},{16,17},{18,... | collective-permute-start | bytes 26120 | tf_op jit(solution)/shard_map/ppermute | solution.py:157
  24.2 4.3 %slice-start.1 = ((s8[8388608]{0:T(1024)(128)(4,1)}), s8[4194304]{0:T(1024)(128)(4,1)S(1)}, s32[]{:S(2)}) async-start(s8[8388608]{0:T(1024)(128)(4,1)} %bitcast.116), calls=%async_computation.5 | async-start | bytes 8388608
  28.4 25.5 %copy-start.9 = (f32[128]{0:T(128)S(1)}, f32[128]{0:T(128)}, u32[]{:S(2)}) copy-start(f32[128]{0:T(128)} %param.20) | copy-start | bytes 1540
  28.4 25.5 %copy-start.10 = (f32[128]{0:T(128)S(1)}, f32[128]{0:T(128)}, u32[]{:S(2)}) copy-start(f32[128]{0:T(128)} %param.19) | copy-start | bytes 1540
  58.0 52.9 %all-to-all-start = ((bf16[16,2,4,64,128]{4,3,2,1,0:T(8,128)(2,1)}), bf16[16,2,4,64,128]{4,3,2,1,0:T(8,128)(2,1)}, u32[]{:S(2)}, u32[]{:S(2)}) async-start(bf16[16,2,4,64,128]{4,3,2,1,0:T(8,128)(2,1)} %bitcast.122), calls=%async_computation | async-start | bytes 4194304 | tf_op jit(solution)/shard_map/all_to_all | solution.py:220
  63.4 3.5 %copy-start.6 = (bf16[32,512,128]{2,1,0:T(8,128)(2,1)S(1)}, bf16[32,512,128]{2,1,0:T(8,128)(2,1)}, u32[]{:S(2)}) copy-start(bf16[32,512,128]{2,1,0:T(8,128)(2,1)} %param.12) | copy-start | bytes 12582916
  91.6 2.5 copy-start.2
  91.6 24.3 %copy-start.8 = (f32[4,225]{1,0:T(4,128)S(1)}, f32[4,225]{1,0:T(4,128)}, u32[]{:S(2)}) copy-start(f32[4,225]{1,0:T(4,128)} %param.22) | copy-start | bytes 10804
  110.9 52.4 %all-to-all-start.2 = ((bf16[16,2,4,64,128]{4,3,2,1,0:T(8,128)(2,1)}), bf16[16,2,4,64,128]{4,3,2,1,0:T(8,128)(2,1)}, u32[]{:S(2)}, u32[]{:S(2)}) async-start(bf16[16,2,4,64,128]{4,3,2,1,0:T(8,128)(2,1)} %bitcast.123), calls=%async_computation.2 | async-start | bytes 4194304 | tf_op jit(solution)/shard_map/all_to_all | solution.py:220
  163.3 52.4 %all-to-all-start.1 = ((bf16[16,2,4,64,128]{4,3,2,1,0:T(8,128)(2,1)}), bf16[16,2,4,64,128]{4,3,2,1,0:T(8,128)(2,1)}, u32[]{:S(2)}, u32[]{:S(2)}) async-start(bf16[16,2,4,64,128]{4,3,2,1,0:T(8,128)(2,1)} %bitcast.124), calls=%async_computation.1 | async-start | bytes 4194304 | tf_op jit(solution)/shard_map/all_to_all | solution.py:232
  188.9 81.3 %copy-start.4 = (bf16[128,128]{1,0:T(8,128)(2,1)S(1)}, bf16[128,128]{1,0:T(8,128)(2,1)}, u32[]{:S(2)}) copy-start(bf16[128,128]{1,0:T(8,128)(2,1)} %param.23) | copy-start | bytes 98308
  215.8 52.4 %all-to-all-start.3 = ((bf16[16,2,4,64,128]{4,3,2,1,0:T(8,128)(2,1)}), bf16[16,2,4,64,128]{4,3,2,1,0:T(8,128)(2,1)}, u32[]{:S(2)}, u32[]{:S(2)}) async-start(bf16[16,2,4,64,128]{4,3,2,1,0:T(8,128)(2,1)} %bitcast.125), calls=%async_computation.3 | async-start | bytes 4194304 | tf_op jit(solution)/shard_map/all_to_all | solution.py:232
  268.2 4.3 %copy-start.3 = (bf16[16,512,128]{2,1,0:T(8,128)(2,1)S(1)}, bf16[16,512,128]{2,1,0:T(8,128)(2,1)}, u32[]{:S(2)}) copy-start(bf16[16,512,128]{2,1,0:T(8,128)(2,1)} %copy-done.2) | copy-start | bytes 6291460
  270.1 5.4 %copy-start.1 = (bf16[128,256]{1,0:T(8,128)(2,1)S(1)}, bf16[128,256]{1,0:T(8,128)(2,1)}, u32[]{:S(2)}) copy-start(bf16[128,256]{1,0:T(8,128)(2,1)} %param.13) | copy-start | bytes 196612

commit v4 on v0

--- a/solution.py
+++ b/solution.py
@@ -160,14 +160,15 @@
         ]
     )[:, None, None]
 
-    def grown(cells, valid):
-        return jnp.where(valid, expand_layer(cells, expand_weight, expand_bias), jnp.zeros((), jnp.bfloat16))
-
+    width, height = top.shape[1], left.shape[0]
+    cells = jnp.concatenate([top[0], bottom[0], left[:, 0], right[:, 0]], axis=0)
+    grown = expand_layer(cells, expand_weight, expand_bias)
+    zero = jnp.zeros((), jnp.bfloat16)
     return (
-        grown(top, row_at > 0),
-        grown(bottom, row_at < row_size - 1),
-        grown(left, row_ok & (col_at > 0)),
-        grown(right, row_ok & (col_at < col_size - 1)),
+        jnp.where(row_at > 0, grown[:width], zero)[None],
+        jnp.where(row_at < row_size - 1, grown[width : 2 * width], zero)[None],
+        jnp.where(row_ok & (col_at > 0), grown[2 * width : 2 * width + height][:, None], zero),
+        jnp.where(row_ok & (col_at < col_size - 1), grown[2 * width + height :][:, None], zero),
     )
 
 

time: 276 us -> 277 us (level)
    dot_general x5 -> x2, matrix products: 11.7 us -> 11.2 us  [expand_layer(): jnp.dot(features, expand_weight, preferred_element_type=jnp.float32)]
  transfers between devices with their start and end apart: 8 -> 8, of which waited for: 4 -> 5; matrix products, arithmetic and copies ran while one was open for 33% -> 31% of each run, Pallas kernels for 12% -> 12%
where the time goes in v4:
time: 277 us; the launch traced here: 276 us
  waiting for transfers between devices  83.3 us (30%)
  matrix products  60.4 us (22%)
  local copies, waits for them, and re-layouts  50.7 us (18%)
  Pallas kernels  32 us (12%)
  starting transfers between devices  30.6 us (11%)
  other arithmetic  18.9 us (7%)
    all_to_all x2, waiting for transfers between devices, body(): returned = lax.all_to_all(returned, ('row', 'col'), 0, 0, tiled=True)  65.8 us
    dot_general x2, matrix products, body(): jnp.dot(hidden, project_weight, preferred_element_type=jnp.float32)  47.8 us
    pallas_call x2, Pallas kernels, grid_attention(): pl.pallas_call(attention_kernel, grid=(count // block,), in_specs=[pl.Blo...  32 us
    all_to_all x2, waiting for transfers between devices, body(): moved = lax.all_to_all(pair, ('row', 'col'), 0, 0, tiled=True)  16.8 us
    gather x2, local copies, waits for them, and re-layouts, grid_bias(): return jnp.take(position_bias, offset_index, axis=1)  16.5 us
    dot_general x2, matrix products, expand_layer(): jnp.dot(features, expand_weight, preferred_element_type=jnp.float32)  11.2 us
    transpose x2, local copies, waits for them, and re-layouts, body(): returned = heads_out.reshape(sub, pp, inner_cols, G, col_size, across, ch...  10.8 us
    all_to_all x2, starting transfers between devices, body(): moved = lax.all_to_all(pair, ('row', 'col'), 0, 0, tiled=True)  10.1 us
  transfers between devices with their start and end apart: 8, of which 5 were waited for; matrix products, arithmetic and copies ran while one was open for 31% of the time, Pallas kernels for 12%

profile of v4, /device:TPU:13, one launch (start us, length us, event | category | flops | bytes accessed | tf_op | source)
XLA Modules:
  0.0 276.4 jit_solution(18133046971439798458)
XLA Ops:
  1.0 2.1 collective-permute-start.1
  3.2 4.0 %collective-permute-start = (bf16[512,128]{1,0:T(8,128)(2,1)S(1)}, bf16[512,128]{1,0:T(8,128)(2,1)S(1)}, u32[]{:S(2)}, u32[]{:S(2)}) collective-permute-start(bf16[512,128]{1,0:T(8,128)(2,1)S(1)} %get-tuple-element.12), channel_id=1, source_target_pairs={{0,2},{2,4},{4,6},{6,8},{8,10},{10,12},{12,14},{1,3},{3,5},{5,7},{... | collective-permute-start | bytes 393224 | tf_op jit(solution)/shard_map/ppermute | solution.py:148
  8.2 10.7 %fusion.7 = bf16[32,512,256]{2,1,0:T(8,128)(2,1)} fusion(bf16[32,512,128]{2,1,0:T(8,128)(2,1)} %param.12, f32[256]{0:T(256)} %param.14, bf16[128,256]{1,0:T(8,128)(2,1)S(1)} %copy-done), kind=kOutput, calls=%fused_computation.9 | convolution fusion | flops 1115684864 | bytes 12649472 | tf_op jit(solution)/shard_map/dot_general | solution.py:30
  20.3 3.1 %collective-permute-start.3 = (bf16[34,128]{1,0:T(8,128)(2,1)S(1)}, bf16[34,128]{1,0:T(8,128)(2,1)S(1)}, u32[]{:S(2)}, u32[]{:S(2)}) collective-permute-start(bf16[34,128]{1,0:T(8,128)(2,1)S(1)} %pad_maximum_fusion.8), channel_id=1, source_target_pairs={{1,0},{3,2},{5,4},{7,6},{9,8},{11,10},{13,12},{15,14},{17,16},{19,... | collective-permute-start | bytes 26120 | tf_op jit(solution)/shard_map/ppermute | solution.py:154
  25.3 3.0 %fusion.29 = bf16[18,512,256]{2,1,0:T(8,128)(2,1)S(1)} fusion(bf16[1,512,256]{2,1,0:T(8,128)(2,1)S(1)} %get-tuple-element.14, bf16[32,512,256]{2,1,0:T(8,128)(2,1)} %fusion.7), kind=kLoop, calls=%fused_computation.51 | loop fusion | flops 2359296 | bytes 13369344 | tf_op jit(solution)/shard_map/concatenate | solution.py:137
  30.7 23.1 %convert_reduce_fusion.1 = (f32[16,512]{1,0:T(8,128)S(1)}, bf16[16,512,128]{2,1,0:T(8,128)(2,1)S(1)}) fusion(f32[128]{0:T(128)S(1)} %copy-done.15, bf16[256,128]{1,0:T(8,128)(2,1)S(1)} %copy-done.12, bf16[18,512,256]{2,1,0:T(8,128)(2,1)S(1)} %fusion.29, bf16[18,1,256]{2,1,0:T(2,128)(2,1)S(1)} %copy.22, bf16[18,1,256]{2,1,0:T(2,128)(2,1)S(1)} %copy.21, ...), kind=kOutput, calls=%fused_computation.45 | convolution fusion | flops 662691840 | bytes 26098176 | tf_op jit(solution)/shard_map/dot_general | solution.py:210
  53.9 2.4 fusion.42
  56.3 2.5 fusion.45
  58.8 1.5 copy.23
  60.3 5.2 %all-to-all-start = ((bf16[16,2,4,64,128]{4,3,2,1,0:T(8,128)(2,1)}), bf16[16,2,4,64,128]{4,3,2,1,0:T(8,128)(2,1)}, u32[]{:S(2)}, u32[]{:S(2)}) async-start(bf16[16,2,4,64,128]{4,3,2,1,0:T(8,128)(2,1)} %bitcast.109), calls=%async_computation | async-start | bytes 4194304 | tf_op jit(solution)/shard_map/all_to_all | solution.py:217
  65.5 2.7 fusion.28
  69.1 24.7 %convert_reduce_fusion = (f32[16,512]{1,0:T(8,128)S(1)}, bf16[16,512,128]{2,1,0:T(8,128)(2,1)S(1)}) fusion(f32[128]{0:T(128)S(1)} %copy-done.15, bf16[256,128]{1,0:T(8,128)(2,1)S(1)} %copy-done.12, bf16[18,512,256]{2,1,0:T(8,128)(2,1)S(1)} %fusion.28, bf16[18,1,256]{2,1,0:T(2,128)(2,1)S(1)} %copy.30, bf16[18,1,256]{2,1,0:T(2,128)(2,1)S(1)} %copy.29, ...), kind=kOutput, calls=%fused_computation.42 | convolution fusion | flops 662691840 | bytes 26079744 | tf_op jit(solution)/shard_map/dot_general | solution.py:210
  93.8 2.4 fusion.38
  96.2 2.5 fusion.41
  100.2 12.8 %all-to-all-done = bf16[16,2,4,64,128]{4,3,2,1,0:T(8,128)(2,1)} async-done(((bf16[16,2,4,64,128]{4,3,2,1,0:T(8,128)(2,1)}), bf16[16,2,4,64,128]{4,3,2,1,0:T(8,128)(2,1)}, u32[]{:S(2)}, u32[]{:S(2)}) %all-to-all-start) | async-done | bytes 2097184 | tf_op jit(solution)/shard_map/all_to_all | solution.py:217
  113.1 4.9 %all-to-all-start.2 = ((bf16[16,2,4,64,128]{4,3,2,1,0:T(8,128)(2,1)}), bf16[16,2,4,64,128]{4,3,2,1,0:T(8,128)(2,1)}, u32[]{:S(2)}, u32[]{:S(2)}) async-start(bf16[16,2,4,64,128]{4,3,2,1,0:T(8,128)(2,1)} %bitcast.108), calls=%async_computation.2 | async-start | bytes 4194304 | tf_op jit(solution)/shard_map/all_to_all | solution.py:217
  118.3 14.2 %gather_fusion = f32[4096,4]{1,0:T(8,128)} fusion(f32[4,225]{0,1:T(8,128)S(1)} %copy.25, s32[4096]{0:T(1024)S(1)} %broadcast_clamp_fusion), kind=kCustom, calls=%fused_computation | custom fusion | bytes 147456 | tf_op jit(solution)/shard_map/jit(_take)/gather | solution.py:62
  132.5 2.3 copy.35
  135.6 4.6 %copy.24 = bf16[8,1,2,2,4,64,128]{6,4,2,0,5,3,1:T(4,128)(2,1)} copy(bf16[8,1,2,2,4,64,128]{6,5,4,3,2,0,1:T(8,128)(2,1)} %bitcast.29) | data formatting | bytes 4194304 | tf_op jit(solution)/shard_map/reshape | solution.py:219
  140.2 16.0 %shard_map.118 = bf16[128,64,128]{2,1,0:T(8,128)(2,1)} custom-call(bf16[128,64,128]{2,1,0:T(8,128)(2,1)} %bitcast.114, bf16[128,384]{1,0:T(8,128)(2,1)} %w_ref.3, f32[4,64,64]{2,1,0:T(8,128)} %select_bitcast_fusion.bias_ref), custom_call_target="tpu_custom_call" | custom-call | tf_op jit(solution)/shard_map/pallas_call | solution.py:112
  156.2 5.4 %copy.27 = bf16[8,1,2,2,4,64,128]{6,5,4,3,2,0,1:T(8,128)(2,1)} copy(bf16[8,1,2,2,4,64,128]{6,4,2,0,5,3,1:T(4,128)(2,1)} %bitcast.115) | data formatting | bytes 4194304 | tf_op jit(solution)/shard_map/transpose | solution.py:226
  161.6 3.9 %all-to-all-done.2 = bf16[16,2,4,64,128]{4,3,2,1,0:T(8,128)(2,1)} async-done(((bf16[16,2,4,64,128]{4,3,2,1,0:T(8,128)(2,1)}), bf16[16,2,4,64,128]{4,3,2,1,0:T(8,128)(2,1)}, u32[]{:S(2)}, u32[]{:S(2)}) %all-to-all-start.2) | async-done | bytes 2097184 | tf_op jit(solution)/shard_map/all_to_all | solution.py:217
  165.5 4.9 %all-to-all-start.1 = ((bf16[16,2,4,64,128]{4,3,2,1,0:T(8,128)(2,1)}), bf16[16,2,4,64,128]{4,3,2,1,0:T(8,128)(2,1)}, u32[]{:S(2)}, u32[]{:S(2)}) async-start(bf16[16,2,4,64,128]{4,3,2,1,0:T(8,128)(2,1)} %bitcast.110), calls=%async_computation.1 | async-start | bytes 4194304 | tf_op jit(solution)/shard_map/all_to_all | solution.py:229
  170.4 4.6 %copy.32 = bf16[8,1,2,2,4,64,128]{6,4,2,0,5,3,1:T(4,128)(2,1)} copy(bf16[8,1,2,2,4,64,128]{6,5,4,3,2,0,1:T(8,128)(2,1)} %bitcast.47) | data formatting | bytes 4194304 | tf_op jit(solution)/shard_map/reshape | solution.py:219
  175.0 16.0 %shard_map.119 = bf16[128,64,128]{2,1,0:T(8,128)(2,1)} custom-call(bf16[128,64,128]{2,1,0:T(8,128)(2,1)} %bitcast.112, bf16[128,384]{1,0:T(8,128)(2,1)} %w_ref.3, f32[4,64,64]{2,1,0:T(8,128)} %select_bitcast_fusion.bias_ref), custom_call_target="tpu_custom_call" | custom-call | tf_op jit(solution)/shard_map/pallas_call | solution.py:112
  191.0 5.4 %copy.33 = bf16[8,1,2,2,4,64,128]{6,5,4,3,2,0,1:T(8,128)(2,1)} copy(bf16[8,1,2,2,4,64,128]{6,4,2,0,5,3,1:T(4,128)(2,1)} %bitcast.113) | data formatting | bytes 4194304 | tf_op jit(solution)/shard_map/transpose | solution.py:226
  196.4 21.6 %all-to-all-done.1 = bf16[16,2,4,64,128]{4,3,2,1,0:T(8,128)(2,1)} async-done(((bf16[16,2,4,64,128]{4,3,2,1,0:T(8,128)(2,1)}), bf16[16,2,4,64,128]{4,3,2,1,0:T(8,128)(2,1)}, u32[]{:S(2)}, u32[]{:S(2)}) %all-to-all-start.1) | async-done | bytes 2097184 | tf_op jit(solution)/shard_map/all_to_all | solution.py:229
  217.9 4.9 %all-to-all-start.3 = ((bf16[16,2,4,64,128]{4,3,2,1,0:T(8,128)(2,1)}), bf16[16,2,4,64,128]{4,3,2,1,0:T(8,128)(2,1)}, u32[]{:S(2)}, u32[]{:S(2)}) async-start(bf16[16,2,4,64,128]{4,3,2,1,0:T(8,128)(2,1)} %bitcast.111), calls=%async_computation.3 | async-start | bytes 4194304 | tf_op jit(solution)/shard_map/all_to_all | solution.py:229
  222.8 3.2 %copy.28 = bf16[8,2,4,2,64,128]{5,4,3,2,1,0:T(8,128)(2,1)} copy(bf16[8,2,4,2,64,128]{5,4,2,1,3,0:T(8,128)(2,1)} %bitcast.38) | data formatting | bytes 4194304 | tf_op jit(solution)/shard_map/transpose | solution.py:232
  226.1 44.3 %all-to-all-done.3 = bf16[16,2,4,64,128]{4,3,2,1,0:T(8,128)(2,1)} async-done(((bf16[16,2,4,64,128]{4,3,2,1,0:T(8,128)(2,1)}), bf16[16,2,4,64,128]{4,3,2,1,0:T(8,128)(2,1)}, u32[]{:S(2)}, u32[]{:S(2)}) %all-to-all-start.3) | async-done | bytes 2097184 | tf_op jit(solution)/shard_map/all_to_all | solution.py:229
  270.4 1.9 copy.34
  274.0 2.4 pad_maximum_fusion.6
  (76 shorter events, 12.6 us)
Async XLA Ops:
  0.0 8.2 %copy-start = (bf16[128,256]{1,0:T(8,128)(2,1)S(1)}, bf16[128,256]{1,0:T(8,128)(2,1)}, u32[]{:S(2)}) copy-start(bf16[128,256]{1,0:T(8,128)(2,1)} %param.13) | copy-start | bytes 196612
  1.0 17.9 %collective-permute-start.1 = (bf16[512,128]{1,0:T(8,128)(2,1)S(1)}, bf16[512,128]{1,0:T(8,128)(2,1)S(1)}, u32[]{:S(2)}, u32[]{:S(2)}) collective-permute-start(bf16[512,128]{1,0:T(8,128)(2,1)S(1)} %get-tuple-element.11), channel_id=1, source_target_pairs={{2,0},{4,2},{6,4},{8,6},{10,8},{12,10},{14,12},{3,1},{5,3},{7,5},{... | collective-permute-start | bytes 393224 | tf_op jit(solution)/shard_map/ppermute | solution.py:149
  3.2 15.7 %collective-permute-start = (bf16[512,128]{1,0:T(8,128)(2,1)S(1)}, bf16[512,128]{1,0:T(8,128)(2,1)S(1)}, u32[]{:S(2)}, u32[]{:S(2)}) collective-permute-start(bf16[512,128]{1,0:T(8,128)(2,1)S(1)} %get-tuple-element.12), channel_id=1, source_target_pairs={{0,2},{2,4},{4,6},{6,8},{8,10},{10,12},{12,14},{1,3},{3,5},{5,7},{... | collective-permute-start | bytes 393224 | tf_op jit(solution)/shard_map/ppermute | solution.py:148
  8.2 10.7 %copy-start.8 = (f32[3,3,256]{2,1,0:T(4,128)S(1)}, f32[3,3,256]{2,1,0:T(4,128)}, u32[]{:S(2)}) copy-start(f32[3,3,256]{2,1,0:T(4,128)} %param.15) | copy-start | bytes 27652
  8.2 16.3 %copy-start.13 = (f32[256]{0:T(256)S(1)}, f32[256]{0:T(256)}, u32[]{:S(2)}) copy-start(f32[256]{0:T(256)} %param.14) | copy-start | bytes 3076
  18.9 4.6 %collective-permute-start.2 = (bf16[34,128]{1,0:T(8,128)(2,1)S(1)}, bf16[34,128]{1,0:T(8,128)(2,1)S(1)}, u32[]{:S(2)}, u32[]{:S(2)}) collective-permute-start(bf16[34,128]{1,0:T(8,128)(2,1)S(1)} %pad_maximum_fusion.7), channel_id=1, source_target_pairs={{0,1},{2,3},{4,5},{6,7},{8,9},{10,11},{12,13},{14,15},{16,17},{18,... | collective-permute-start | bytes 26120 | tf_op jit(solution)/shard_map/ppermute | solution.py:153
  20.3 3.9 %collective-permute-start.3 = (bf16[34,128]{1,0:T(8,128)(2,1)S(1)}, bf16[34,128]{1,0:T(8,128)(2,1)S(1)}, u32[]{:S(2)}, u32[]{:S(2)}) collective-permute-start(bf16[34,128]{1,0:T(8,128)(2,1)S(1)} %pad_maximum_fusion.8), channel_id=1, source_target_pairs={{1,0},{3,2},{5,4},{7,6},{9,8},{11,10},{13,12},{15,14},{17,16},{19,... | collective-permute-start | bytes 26120 | tf_op jit(solution)/shard_map/ppermute | solution.py:154
  24.5 3.8 %slice-start = ((s8[8388608]{0:T(1024)(128)(4,1)}), s8[4194304]{0:T(1024)(128)(4,1)S(1)}, s32[]{:S(2)}) async-start(s8[8388608]{0:T(1024)(128)(4,1)} %bitcast.102), calls=%async_computation.4 | async-start | bytes 8388608
  25.3 4.2 %slice-start.1 = ((s8[8388608]{0:T(1024)(128)(4,1)}), s8[4194304]{0:T(1024)(128)(4,1)S(1)}, s32[]{:S(2)}) async-start(s8[8388608]{0:T(1024)(128)(4,1)} %bitcast.102), calls=%async_computation.5 | async-start | bytes 8388608
  25.3 5.4 %copy-start.6 = (bf16[32,512,128]{2,1,0:T(8,128)(2,1)S(1)}, bf16[32,512,128]{2,1,0:T(8,128)(2,1)}, u32[]{:S(2)}) copy-start(bf16[32,512,128]{2,1,0:T(8,128)(2,1)} %param.12) | copy-start | bytes 12582916
  25.3 5.4 %copy-start.12 = (bf16[256,128]{1,0:T(8,128)(2,1)S(1)}, bf16[256,128]{1,0:T(8,128)(2,1)}, u32[]{:S(2)}) copy-start(bf16[256,128]{1,0:T(8,128)(2,1)} %param.17) | copy-start | bytes 196612
  25.3 5.4 %copy-start.14 = (f32[256]{0:T(256)S(1)}, f32[256]{0:T(256)}, u32[]{:S(2)}) copy-start(f32[256]{0:T(256)} %param.16) | copy-start | bytes 3076
  25.3 5.4 %copy-start.15 = (f32[128]{0:T(128)S(1)}, f32[128]{0:T(128)}, u32[]{:S(2)}) copy-start(f32[128]{0:T(128)} %param.18) | copy-start | bytes 1540
  30.7 25.6 %copy-start.10 = (f32[128]{0:T(128)S(1)}, f32[128]{0:T(128)}, u32[]{:S(2)}) copy-start(f32[128]{0:T(128)} %param.20) | copy-start | bytes 1540
  30.7 25.6 %copy-start.11 = (f32[128]{0:T(128)S(1)}, f32[128]{0:T(128)}, u32[]{:S(2)}) copy-start(f32[128]{0:T(128)} %param.19) | copy-start | bytes 1540
  60.3 52.7 %all-to-all-start = ((bf16[16,2,4,64,128]{4,3,2,1,0:T(8,128)(2,1)}), bf16[16,2,4,64,128]{4,3,2,1,0:T(8,128)(2,1)}, u32[]{:S(2)}, u32[]{:S(2)}) async-start(bf16[16,2,4,64,128]{4,3,2,1,0:T(8,128)(2,1)} %bitcast.109), calls=%async_computation | async-start | bytes 4194304 | tf_op jit(solution)/shard_map/all_to_all | solution.py:217
  65.5 3.5 %copy-start.7 = (bf16[32,512,128]{2,1,0:T(8,128)(2,1)S(1)}, bf16[32,512,128]{2,1,0:T(8,128)(2,1)}, u32[]{:S(2)}) copy-start(bf16[32,512,128]{2,1,0:T(8,128)(2,1)} %param.12) | copy-start | bytes 12582916
  93.7 2.4 copy-start.2
  98.7 19.4 %copy-start.9 = (f32[4,225]{1,0:T(4,128)S(1)}, f32[4,225]{1,0:T(4,128)}, u32[]{:S(2)}) copy-start(f32[4,225]{1,0:T(4,128)} %param.22) | copy-start | bytes 10804
  113.1 52.4 %all-to-all-start.2 = ((bf16[16,2,4,64,128]{4,3,2,1,0:T(8,128)(2,1)}), bf16[16,2,4,64,128]{4,3,2,1,0:T(8,128)(2,1)}, u32[]{:S(2)}, u32[]{:S(2)}) async-start(bf16[16,2,4,64,128]{4,3,2,1,0:T(8,128)(2,1)} %bitcast.108), calls=%async_computation.2 | async-start | bytes 4194304 | tf_op jit(solution)/shard_map/all_to_all | solution.py:217
  165.5 52.4 %all-to-all-start.1 = ((bf16[16,2,4,64,128]{4,3,2,1,0:T(8,128)(2,1)}), bf16[16,2,4,64,128]{4,3,2,1,0:T(8,128)(2,1)}, u32[]{:S(2)}, u32[]{:S(2)}) async-start(bf16[16,2,4,64,128]{4,3,2,1,0:T(8,128)(2,1)} %bitcast.110), calls=%async_computation.1 | async-start | bytes 4194304 | tf_op jit(solution)/shard_map/all_to_all | solution.py:229
  217.9 52.4 %all-to-all-start.3 = ((bf16[16,2,4,64,128]{4,3,2,1,0:T(8,128)(2,1)}), bf16[16,2,4,64,128]{4,3,2,1,0:T(8,128)(2,1)}, u32[]{:S(2)}, u32[]{:S(2)}) async-start(bf16[16,2,4,64,128]{4,3,2,1,0:T(8,128)(2,1)} %bitcast.111), calls=%async_computation.3 | async-start | bytes 4194304 | tf_op jit(solution)/shard_map/all_to_all | solution.py:229
  222.8 49.5 %copy-start.5 = (bf16[128,128]{1,0:T(8,128)(2,1)S(1)}, bf16[128,128]{1,0:T(8,128)(2,1)}, u32[]{:S(2)}) copy-start(bf16[128,128]{1,0:T(8,128)(2,1)} %param.23) | copy-start | bytes 98308
  270.4 2.2 copy-start.4
  270.4 2.9 %copy-start.3 = (bf16[16,512,128]{2,1,0:T(8,128)(2,1)S(1)}, bf16[16,512,128]{2,1,0:T(8,128)(2,1)}, u32[]{:S(2)}) copy-start(bf16[16,512,128]{2,1,0:T(8,128)(2,1)} %copy-done.2) | copy-start | bytes 6291460
  273.3 3.1 %copy-start.1 = (bf16[128,256]{1,0:T(8,128)(2,1)S(1)}, bf16[128,256]{1,0:T(8,128)(2,1)}, u32[]{:S(2)}) copy-start(bf16[128,256]{1,0:T(8,128)(2,1)} %param.13) | copy-start | bytes 196612
